TPU v7x, 1024 devices: a whole 4x8x16 slice. The times are simulated.
1024 devices in a mesh: dp: 16 (over z_lo, x), space: 64 (over y, z_hi, core).
Axes of the slice: x: 4, y: 8, z: 16 (z_hi: 4, z_lo: 4; z = z_hi * 4 + z_lo), core: 2. Of those that a mesh axis runs over, the one named last changes fastest.
Arguments:
- volume: bfloat16 [16, 32, 128, 16, 128], P('dp', None, 'space'), may hold values from -6 to 6
- kernel: bfloat16 [64, 32, 3, 3, 3], replicated, may hold values from -0.21875 to 0.21875
- cotangent: bfloat16 [16, 64, 64, 8, 64], P('dp', None, 'space'), may hold values from -6 to 6
Outputs:
- activated: bfloat16 [16, 64, 64, 8, 64], P('dp', None, 'space')
- grad_volume: bfloat16 [16, 32, 128, 16, 128], P('dp', None, 'space')
- grad_kernel: float32 [64, 32, 3, 3, 3], replicated
All inputs are finite; a program needn't handle non-finite values.
Results may differ from a plain program's by a relative error of at most 0.0049.
Values may be sent and summed in bfloat16 or wider, within the bound.
No kernel may reach another device: no remote copies, remote signals or barrier semaphores. Data moves between devices by JAX's collectives and lax.ppermute only.
A program may use at most 64 MiB of HBM per device.

v0:
```python
import jax
import jax.numpy as jnp
from jax import lax
from jax.sharding import PartitionSpec as P


def from_behind(block, axis, distance):
    devices = range(lax.axis_size(axis))
    route = [(i - distance, i) for i in devices if i - distance in devices]
    return lax.ppermute(block, axis, route)


def in_blocks(x, dim, devices):
    dims = x.shape
    parts = x.reshape(*dims[:dim], devices, dims[dim] // devices, *dims[dim + 1 :])
    return jnp.moveaxis(parts, dim, 0)


def summed_on_arrival(x, axis, dim):
    parts = in_blocks(x, dim, lax.axis_size(axis))
    arrived = lax.all_to_all(parts, axis, split_axis=0, concat_axis=0, tiled=True)
    return arrived.sum(axis=0)


def sent_to_all(x, axis):
    copies = jnp.broadcast_to(x, (lax.axis_size(axis), *x.shape))
    return lax.all_to_all(copies, axis, split_axis=0, concat_axis=0, tiled=True)


def taken_together(x, axis):
    everything = sent_to_all(x, axis)
    return jnp.sum(everything, axis=0)


def laid_out(parts, dim):
    parts = jnp.moveaxis(parts, 0, dim)
    dims = parts.shape
    return parts.reshape(*dims[:dim], dims[dim] * dims[dim + 1], *dims[dim + 2 :])


def gathered_copies(x, axis, dim):
    parts = sent_to_all(x, axis)
    return laid_out(parts, dim)


def convolve(inputs, weights, low, high):
    return lax.conv_general_dilated(
        inputs,
        weights,
        (2, 2, 2),
        [(low, high), (1, 1), (1, 1)],
        dimension_numbers=("NCDHW", "OIDHW", "NCDHW"),
        preferred_element_type=jnp.float32,
    )


def input_grad(grads, weights, low, high):
    flipped = weights[:, :, ::-1, ::-1, ::-1]
    return lax.conv_general_dilated(
        grads,
        flipped,
        (1, 1, 1),
        [(low, high), (1, 2), (1, 2)],
        lhs_dilation=(2, 2, 2),
        dimension_numbers=("NCDHW", "IODHW", "NCDHW"),
        preferred_element_type=jnp.float32,
    )


def weight_grad(inputs, grads):
    return lax.conv_general_dilated(
        inputs,
        grads,
        (1, 1, 1),
        [(0, 0), (1, 0), (1, 0)],
        rhs_dilation=(2, 2, 2),
        dimension_numbers=("CNDHW", "IODHW", "CNDHW"),
        preferred_element_type=jnp.float32,
    )


def per_device(volume, kernel, cotangent):
    below = from_behind(volume[:, :, -1:], "space", 1)
    extended = jnp.concatenate([below, volume], axis=2)
    pre = convolve(extended, kernel, 0, 0)
    activated = (0.01 * pre + 0.99 * jax.nn.softplus(pre)).astype(jnp.bfloat16)
    local_grad = (cotangent.astype(jnp.float32) * (0.01 + 0.99 * jax.nn.sigmoid(pre))).astype(
        jnp.bfloat16
    )
    grad_extended = input_grad(local_grad, kernel, 2, 2)
    kernel_local = weight_grad(extended, local_grad)
    grad_input = grad_extended[:, :, 1:]
    next_grad = from_behind(local_grad[:, :, :1], "space", -1)
    from_above = input_grad(next_grad, kernel, 2, 0)
    grad_input = grad_input.at[:, :, -1:].add(from_above)
    flat_terms = kernel_local.reshape(-1)
    share = summed_on_arrival(flat_terms, "space", 0)
    share = taken_together(share, "dp")
    kernel_total = gathered_copies(share, "space", 0).reshape(kernel_local.shape)
    total_cells = (
        volume.shape[0]
        * lax.axis_size("dp")
        * volume.shape[2]
        * lax.axis_size("space")
        * volume.shape[3]
        * volume.shape[4]
        / 8.0
    )
    grad_kernel = kernel_total / jnp.sqrt(jnp.float32(total_cells))
    return (activated, grad_input.astype(jnp.bfloat16), grad_kernel)


def solution(mesh):
    placed = (P("dp", None, "space", None, None), P(), P("dp", None, "space", None, None))
    return jax.shard_map(
        per_device,
        mesh=mesh,
        in_specs=placed,
        out_specs=(P("dp", None, "space", None, None), P("dp", None, "space", None, None), P()),
        check_vma=False,
    )
```

profile of v0, /device:TPU:65, one launch (start us, length us, event | category | flops | bytes accessed | tf_op | source)
XLA Modules:
  0.0 128.2 jit_solution(17070995528144501461)
XLA Ops:
  0.6 0.0 copy-start
  0.6 1.0 slice.40
  1.6 11.2 %collective-permute-start = (bf16[1,32,1,16,128]{4,3,2,1,0:T(8,128)(2,1)S(1)}, bf16[1,32,1,16,128]{4,3,2,1,0:T(8,128)(2,1)S(1)}, u32[]{:S(2)}, u32[]{:S(2)}) collective-permute-start(bf16[1,32,1,16,128]{4,3,2,1,0:T(8,128)(2,1)S(1)} %slice.40), channel_id=1, source_target_pairs={{0,1},{1,2},{2,3},{3,4},{4,5},{5,6},{6,7},{7,8},{8,9},{9,10},{10,1... | collective-permute-start | bytes 393224 | tf_op jit(solution)/shard_map/ppermute | solution.py:10
  12.8 1.1 copy.98
  13.9 1.3 %collective-permute-done = bf16[1,32,1,16,128]{4,3,2,1,0:T(8,128)(2,1)S(1)} collective-permute-done((bf16[1,32,1,16,128]{4,3,2,1,0:T(8,128)(2,1)S(1)}, bf16[1,32,1,16,128]{4,3,2,1,0:T(8,128)(2,1)S(1)}, u32[]{:S(2)}, u32[]{:S(2)}) %collective-permute-start) | collective-permute-done | bytes 131104 | tf_op jit(solution)/shard_map/ppermute | solution.py:10
  15.2 1.0 constant_dynamic-update-slice_fusion
  16.2 3.6 %copy.107 = bf16[1,32,3,16,128]{1,0,4,3,2:T(2,128)(2,1)} copy(bf16[1,32,3,16,128]{4,3,2,1,0:T(8,128)(2,1)S(1)} %constant_dynamic-update-slice_fusion) | data formatting | bytes 786432 | tf_op jit(solution)/shard_map/concatenate | solution.py:84
  19.8 1.2 copy.118
  21.0 0.3 pad.2.clone
  21.3 0.0 copy-start.3
  21.3 0.7 copy.96
  22.0 0.1 slice.51
  22.1 0.0 copy-done
  22.1 0.0 copy-done.3
  22.1 0.0 copy-start.1
  22.1 1.3 %multiply_add_fusion = (f32[1,8,8,9,64]{4,2,3,1,0:T(8,128)S(1)}, bf16[1,8,8,9,64]{4,2,3,1,0:T(8,128)(2,1)S(1)}) fusion(bf16[64,32,3,3,3]{0,1,4,3,2:T(8,128)(2,1)S(1)} %copy-done, bf16[32,3,16,1,7,2]{0,4,5,2,1,3:T(8,128)(2,1)S(1)} %slice.51, bf16[32,3,16,1,8,18]{0,4,5,2,1,3:T(8,128)(2,1)S(1)} %copy.96, pred[8,9]{0,1:T(8,128)(4,1)S(1)} %copy-done.3), kind=kOutput, calls=%fused_computation.20 | convolution fusion | flops 63111168 | bytes 817224 | tf_op jit(solution)/shard_map/conv_general_dilated | solution.py:47
  23.4 0.1 copy.99
  23.5 0.5 copy-done.1
  24.0 6.3 %fusion.18 = f32[64,32,3,3,3]{0,1,4,3,2:T(8,128)S(1)} fusion(bf16[1,32,3,16,128]{1,0,4,3,2:T(2,128)(2,1)S(1)} %copy-done.1, bf16[1,64,1,8,64]{1,3,4,0,2:T(8,128)(2,1)S(1)} %fusion.17), kind=kOutput, calls=%fused_computation.24 | convolution fusion | flops 53981184 | bytes 679936 | tf_op jit(solution)/shard_map/conv_general_dilated | solution.py:71
  30.3 0.0 copy-start.2
  30.3 0.3 copy.109
  30.7 0.2 all_to_all.14
  30.9 0.9 copy.110
  31.7 24.4 %all-to-all-start = ((f32[64,1,864]{2,1,0:T(1,128)}), f32[64,1,864]{2,1,0:T(1,128)S(1)}, u32[]{:S(2)}, u32[]{:S(2)}) async-start(f32[64,1,864]{2,1,0:T(1,128)} %copy.110), calls=%async_computation | async-start | bytes 458752 | tf_op jit(solution)/shard_map/all_to_all | solution.py:21
  56.1 2.4 %collective-permute-start.1 = (bf16[1,64,1,8,64]{1,3,4,0,2:T(8,128)(2,1)S(1)}, bf16[1,64,1,8,64]{1,3,4,0,2:T(8,128)(2,1)S(1)}, u32[]{:S(2)}, u32[]{:S(2)}) collective-permute-start(bf16[1,64,1,8,64]{1,3,4,0,2:T(8,128)(2,1)S(1)} %fusion.17), channel_id=1, source_target_pairs={{1,0},{2,1},{3,2},{4,3},{5,4},{6,5},{7,6},{8,7},{9,8},{10,9},{11,1... | collective-permute-start | bytes 196616 | tf_op jit(solution)/shard_map/ppermute | solution.py:10
  58.6 24.9 %all-to-all-done = f32[64,1,864]{2,1,0:T(1,128)S(1)} async-done(((f32[64,1,864]{2,1,0:T(1,128)}), f32[64,1,864]{2,1,0:T(1,128)S(1)}, u32[]{:S(2)}, u32[]{:S(2)}) %all-to-all-start) | async-done | bytes 221216 | tf_op jit(solution)/shard_map/all_to_all | solution.py:21
  83.5 0.2 reduce_sum.18
  83.6 0.7 broadcast_in_dim.6
  84.3 5.2 %all-to-all-start.1 = ((f32[16,1,864]{2,1,0:T(1,128)}), f32[16,1,864]{2,1,0:T(1,128)S(1)}, u32[]{:S(2)}, u32[]{:S(2)}) async-start(f32[16,1,864]{2,1,0:T(1,128)} %broadcast_in_dim.6), calls=%async_computation.1 | async-start | bytes 114688 | tf_op jit(solution)/shard_map/all_to_all | solution.py:27
  89.5 0.0 copy-done.2
  89.5 1.2 convolution_select_fusion
  90.7 1.8 %copy.102 = bf16[2,16,8,18,32]{4,1,3,2,0:T(8,128)(2,1)} copy(f32[2,16,8,18,32]{4,2,3,1,0:T(8,128)S(1)} %convolution_select_fusion) | data formatting | bytes 884736 | tf_op jit(solution)/shard_map/slice | solution.py:92
  92.5 2.8 %all-to-all-done.1 = f32[16,1,864]{2,1,0:T(1,128)S(1)} async-done(((f32[16,1,864]{2,1,0:T(1,128)}), f32[16,1,864]{2,1,0:T(1,128)S(1)}, u32[]{:S(2)}, u32[]{:S(2)}) %all-to-all-start.1) | async-done | bytes 55328 | tf_op jit(solution)/shard_map/all_to_all | solution.py:27
  95.3 0.8 broadcast_in_dim.7
  96.1 5.8 %all-to-all-start.2 = ((f32[64,1,864]{2,1,0:T(1,128)}), f32[64,1,864]{2,1,0:T(1,128)S(1)}, u32[]{:S(2)}, u32[]{:S(2)}) async-start(f32[64,1,864]{2,1,0:T(1,128)} %broadcast_in_dim.7), calls=%async_computation.2 | async-start | bytes 458752 | tf_op jit(solution)/shard_map/all_to_all | solution.py:27
  101.9 2.4 %slice_bitcast_fusion = bf16[1,32,2,16,128]{1,3,4,2,0:T(8,128)(2,1)} fusion(bf16[2,16,1,144,32]{4,1,3,0,2:T(8,128)(2,1)} %bitcast.48), kind=kLoop, calls=%fused_computation.2 | loop fusion | bytes 524288 | tf_op jit(solution)/shard_map/slice | solution.py:92
  104.4 0.8 copy.114
  105.2 0.0 collective-permute-done.1
  105.3 0.8 fusion.5
  106.1 0.2 copy.105
  106.3 0.8 fusion.9
  107.1 2.9 %copy.115 = bf16[1,32,2,16,128]{4,3,2,1,0:T(8,128)(2,1)} copy(bf16[1,32,2,16,128]{1,3,4,2,0:T(8,128)(2,1)} %fusion.9) | data formatting | bytes 524288
  110.1 16.9 %all-to-all-done.2 = f32[64,1,864]{2,1,0:T(1,128)S(1)} async-done(((f32[64,1,864]{2,1,0:T(1,128)}), f32[64,1,864]{2,1,0:T(1,128)S(1)}, u32[]{:S(2)}, u32[]{:S(2)}) %all-to-all-start.2) | async-done | bytes 221216 | tf_op jit(solution)/shard_map/all_to_all | solution.py:27
  127.0 0.2 copy.113
  127.2 0.2 div.14
  127.4 0.8 copy.116
  (12 shorter events, 0.3 us)
Async XLA Ops:
  0.6 21.4 %copy-start = (bf16[64,32,3,3,3]{0,1,4,3,2:T(8,128)(2,1)S(1)}, bf16[64,32,3,3,3]{0,1,4,3,2:T(8,128)(2,1)}, u32[]{:S(2)}) copy-start(bf16[64,32,3,3,3]{0,1,4,3,2:T(8,128)(2,1)} %param.6) | copy-start | bytes 331780
  1.6 13.6 %collective-permute-start = (bf16[1,32,1,16,128]{4,3,2,1,0:T(8,128)(2,1)S(1)}, bf16[1,32,1,16,128]{4,3,2,1,0:T(8,128)(2,1)S(1)}, u32[]{:S(2)}, u32[]{:S(2)}) collective-permute-start(bf16[1,32,1,16,128]{4,3,2,1,0:T(8,128)(2,1)S(1)} %slice.40), channel_id=1, source_target_pairs={{0,1},{1,2},{2,3},{3,4},{4,5},{5,6},{6,7},{7,8},{8,9},{9,10},{10,1... | collective-permute-start | bytes 393224 | tf_op jit(solution)/shard_map/ppermute | solution.py:10
  21.3 0.8 copy-start.3
  22.1 1.9 %copy-start.1 = (bf16[1,32,3,16,128]{1,0,4,3,2:T(2,128)(2,1)S(1)}, bf16[1,32,3,16,128]{1,0,4,3,2:T(2,128)(2,1)}, u32[]{:S(2)}) copy-start(bf16[1,32,3,16,128]{1,0,4,3,2:T(2,128)(2,1)} %copy.107) | copy-start | bytes 1179652
  30.3 59.2 %copy-start.2 = (pred[8,18]{0,1:T(8,128)(4,1)S(1)}, pred[8,18]{0,1:T(8,128)(4,1)}, u32[]{:S(2)}) copy-start(pred[8,18]{0,1:T(8,128)(4,1)} %constant.57) | copy-start | bytes 436
  31.7 51.7 %all-to-all-start = ((f32[64,1,864]{2,1,0:T(1,128)}), f32[64,1,864]{2,1,0:T(1,128)S(1)}, u32[]{:S(2)}, u32[]{:S(2)}) async-start(f32[64,1,864]{2,1,0:T(1,128)} %copy.110), calls=%async_computation | async-start | bytes 458752 | tf_op jit(solution)/shard_map/all_to_all | solution.py:21
  56.1 49.0 %collective-permute-start.1 = (bf16[1,64,1,8,64]{1,3,4,0,2:T(8,128)(2,1)S(1)}, bf16[1,64,1,8,64]{1,3,4,0,2:T(8,128)(2,1)S(1)}, u32[]{:S(2)}, u32[]{:S(2)}) collective-permute-start(bf16[1,64,1,8,64]{1,3,4,0,2:T(8,128)(2,1)S(1)} %fusion.17), channel_id=1, source_target_pairs={{1,0},{2,1},{3,2},{4,3},{5,4},{6,5},{7,6},{8,7},{9,8},{10,9},{11,1... | collective-permute-start | bytes 196616 | tf_op jit(solution)/shard_map/ppermute | solution.py:10
  84.3 11.0 %all-to-all-start.1 = ((f32[16,1,864]{2,1,0:T(1,128)}), f32[16,1,864]{2,1,0:T(1,128)S(1)}, u32[]{:S(2)}, u32[]{:S(2)}) async-start(f32[16,1,864]{2,1,0:T(1,128)} %broadcast_in_dim.6), calls=%async_computation.1 | async-start | bytes 114688 | tf_op jit(solution)/shard_map/all_to_all | solution.py:27
  96.1 30.8 %all-to-all-start.2 = ((f32[64,1,864]{2,1,0:T(1,128)}), f32[64,1,864]{2,1,0:T(1,128)S(1)}, u32[]{:S(2)}, u32[]{:S(2)}) async-start(f32[64,1,864]{2,1,0:T(1,128)} %broadcast_in_dim.7), calls=%async_computation.2 | async-start | bytes 458752 | tf_op jit(solution)/shard_map/all_to_all | solution.py:27
where the time goes:
time: 129 us; the launch traced here: 128 us
  starting transfers between devices  49 us (38%)
  waiting for transfers between devices  45.8 us (36%)
  local copies, waits for them, and re-layouts  22.6 us (18%)
  matrix products  9.64 us (7%)
    all_to_all x1, waiting for transfers between devices, summed_on_arrival(): lax.all_to_all(parts, axis, split_axis=0, concat_axis=0, tiled=True)  24.9 us
    all_to_all x1, starting transfers between devices, summed_on_arrival(): lax.all_to_all(parts, axis, split_axis=0, concat_axis=0, tiled=True)  24.4 us
    all_to_all x2, waiting for transfers between devices, sent_to_all(): return lax.all_to_all(copies, axis, split_axis=0, concat_axis=0, tiled=True)  19.7 us
    ppermute x2, starting transfers between devices, from_behind(): return lax.ppermute(block, axis, route)  13.6 us
    all_to_all x2, starting transfers between devices, sent_to_all(): return lax.all_to_all(copies, axis, split_axis=0, concat_axis=0, tiled=True)  11 us
    unnamed x14, local copies, waits for them, and re-layouts  7.32 us
    conv_general_dilated x1, matrix products, weight_grad(): lax.conv_general_dilated(inputs, grads, (1, 1, 1), [(0, 0), (1, 0), (1, 0...  6.34 us
    concatenate x3, local copies, waits for them, and re-layouts, per_device(): extended = jnp.concatenate([below, volume], axis=2)  4.9 us
  transfers between devices with their start and end apart: 5, of which 4 were waited for; matrix products, arithmetic and copies ran while one was open for 11% of the time, Pallas kernels for 0%

commit v1 on v0

--- a/solution.py
+++ b/solution.py
@@ -93,10 +93,7 @@
     next_grad = from_behind(local_grad[:, :, :1], "space", -1)
     from_above = input_grad(next_grad, kernel, 2, 0)
     grad_input = grad_input.at[:, :, -1:].add(from_above)
-    flat_terms = kernel_local.reshape(-1)
-    share = summed_on_arrival(flat_terms, "space", 0)
-    share = taken_together(share, "dp")
-    kernel_total = gathered_copies(share, "space", 0).reshape(kernel_local.shape)
+    kernel_total = lax.psum(kernel_local, ("dp", "space"))
     total_cells = (
         volume.shape[0]
         * lax.axis_size("dp")

time: 129 us -> 558 us (4.33)
  the two profiles are of different devices: /device:TPU:65 before, /device:TPU:24 now
where the time goes in v1:
time: 558 us; the launch traced here: 557 us
  waiting for transfers between devices  511 us (92%)
  local copies, waits for them, and re-layouts  15.8 us (3%)
  between operations  14.3 us (3%)
  matrix products  10.4 us (2%)
    psum x1, waiting for transfers between devices, per_device(): kernel_total = lax.psum(kernel_local, ('dp', 'space'))  493 us
    ppermute x2, waiting for transfers between devices, from_behind(): return lax.ppermute(block, axis, route)  17.5 us
  transfers between devices with their start and end apart: 3, of which 2 were waited for; matrix products, arithmetic and copies ran while one was open for 3% of the time, Pallas kernels for 0%

profile of v1, /device:TPU:24, one launch (start us, length us, event | category | flops | bytes accessed | tf_op | source)
XLA Modules:
  0.0 557.3 jit_solution(4009672600774955551)
XLA Ops:
  7.2 0.0 copy-start
  7.2 0.0 all-reduce.2.cloned.1.call-start
  7.2 1.0 slice.40
  8.2 1.9 collective-permute-start
  10.1 1.1 copy.32
  11.2 17.5 %collective-permute-done = bf16[1,32,1,16,128]{4,3,2,1,0:T(8,128)(2,1)S(1)} collective-permute-done((bf16[1,32,1,16,128]{4,3,2,1,0:T(8,128)(2,1)S(1)}, bf16[1,32,1,16,128]{4,3,2,1,0:T(8,128)(2,1)S(1)}, u32[]{:S(2)}, u32[]{:S(2)}) %collective-permute-start) | collective-permute-done | bytes 131104 | tf_op jit(solution)/shard_map/ppermute | solution.py:10
  28.7 1.0 constant_dynamic-update-slice_fusion
  29.7 3.6 copy.41
  33.2 1.2 copy.45
  34.4 0.3 pad.2.clone
  34.8 0.0 copy-start.3
  34.8 0.7 copy.30
  35.5 0.1 slice.51
  35.5 0.0 copy-done
  35.5 0.0 copy-done.3
  35.5 1.3 multiply_add_fusion
  36.8 0.0 copy-start.2
  36.8 0.1 copy.33
  37.0 2.1 collective-permute-start.1
  39.2 0.0 copy-done.2
  39.2 1.2 convolution_select_fusion
  40.4 0.0 copy-start.1
  40.4 0.8 copy.36
  41.1 1.2 slice_bitcast_fusion
  42.3 0.0 copy-done.1
  42.3 7.1 %fusion.18 = f32[64,32,3,3,3]{0,1,4,3,2:T(8,128)} fusion(bf16[1,32,3,16,128]{1,0,4,3,2:T(2,128)(2,1)S(1)} %copy-done.1, bf16[1,64,1,8,64]{1,3,4,0,2:T(8,128)(2,1)S(1)} %fusion.17), kind=kOutput, calls=%fused_computation.24 | convolution fusion | flops 53981184 | bytes 679936 | tf_op jit(solution)/shard_map/conv_general_dilated | solution.py:71
  49.4 0.8 copy.43
  50.2 0.0 all-reduce.2.cloned.1.call-update
  50.3 0.0 collective-permute-done.1
  50.4 0.8 fusion.5
  51.2 0.2 copy.39
  51.4 0.8 fusion.9
  52.2 2.9 copy.44
  55.1 493.5 %all-reduce.2.cloned.1.call-done = f32[64,32,3,3,3]{0,1,4,3,2:T(8,128)} async-done(((f32[64,32,3,3,3]{0,1,4,3,2:T(8,128)}), f32[64,32,3,3,3]{0,1,4,3,2:T(8,128)}) %all-reduce.2.cloned.1.call-update) | async-done | bytes 221200 | tf_op jit(solution)/shard_map/psum | solution.py:96
  548.6 1.8 broadcast_multiply_fusion
  (10 shorter events, 0.2 us)
Async XLA Ops:
  7.2 28.4 %copy-start = (bf16[64,32,3,3,3]{0,1,4,3,2:T(8,128)(2,1)S(1)}, bf16[64,32,3,3,3]{0,1,4,3,2:T(8,128)(2,1)}, u32[]{:S(2)}) copy-start(bf16[64,32,3,3,3]{0,1,4,3,2:T(8,128)(2,1)} %param.6) | copy-start | bytes 331780
  7.2 541.4 %all-reduce.2.cloned.1.call-start = ((), (), s32[]{:S(2)}) async-start(), calls=%async_computation | async-start | bytes 884736 | tf_op jit(solution)/shard_map/psum | solution.py:96
  8.2 20.5 %collective-permute-start = (bf16[1,32,1,16,128]{4,3,2,1,0:T(8,128)(2,1)S(1)}, bf16[1,32,1,16,128]{4,3,2,1,0:T(8,128)(2,1)S(1)}, u32[]{:S(2)}, u32[]{:S(2)}) collective-permute-start(bf16[1,32,1,16,128]{4,3,2,1,0:T(8,128)(2,1)S(1)} %slice.40), channel_id=1, source_target_pairs={{0,1},{1,2},{2,3},{3,4},{4,5},{5,6},{6,7},{7,8},{8,9},{9,10},{10,1... | collective-permute-start | bytes 393224 | tf_op jit(solution)/shard_map/ppermute | solution.py:10
  34.8 0.8 copy-start.3
  36.8 2.4 copy-start.2
  37.0 13.3 %collective-permute-start.1 = (bf16[1,64,1,8,64]{1,3,4,0,2:T(8,128)(2,1)S(1)}, bf16[1,64,1,8,64]{1,3,4,0,2:T(8,128)(2,1)S(1)}, u32[]{:S(2)}, u32[]{:S(2)}) collective-permute-start(bf16[1,64,1,8,64]{1,3,4,0,2:T(8,128)(2,1)S(1)} %fusion.17), channel_id=1, source_target_pairs={{1,0},{2,1},{3,2},{4,3},{5,4},{6,5},{7,6},{8,7},{9,8},{10,9},{11,1... | collective-permute-start | bytes 196616 | tf_op jit(solution)/shard_map/ppermute | solution.py:10
  40.4 1.9 copy-start.1
Sparse Core Ops, SparseCore 0:
  50.4 498.1 all-reduce.1

commit v2 on v0

--- a/solution.py
+++ b/solution.py
@@ -79,16 +79,33 @@
     )
 
 
+def patches(extended):
+    planes, high, deep = extended.shape[2] - 1, extended.shape[3], extended.shape[4]
+    padded = jnp.pad(extended[0], ((0, 0), (0, 0), (1, 0), (1, 0)))
+    taps = [
+        padded[:, a : a + planes : 2, b : b + high : 2, d : d + deep : 2]
+        for a in range(3)
+        for b in range(3)
+        for d in range(3)
+    ]
+    cells = jnp.stack(taps, axis=1)
+    return cells.reshape(cells.shape[0] * 27, -1)
+
+
 def per_device(volume, kernel, cotangent):
     below = from_behind(volume[:, :, -1:], "space", 1)
     extended = jnp.concatenate([below, volume], axis=2)
-    pre = convolve(extended, kernel, 0, 0)
+    cells = patches(extended)
+    weights = kernel.reshape(kernel.shape[0], -1)
+    pre = jnp.dot(weights, cells, preferred_element_type=jnp.float32).reshape(cotangent.shape)
     activated = (0.01 * pre + 0.99 * jax.nn.softplus(pre)).astype(jnp.bfloat16)
     local_grad = (cotangent.astype(jnp.float32) * (0.01 + 0.99 * jax.nn.sigmoid(pre))).astype(
         jnp.bfloat16
     )
     grad_extended = input_grad(local_grad, kernel, 2, 2)
-    kernel_local = weight_grad(extended, local_grad)
+    kernel_local = jnp.dot(
+        local_grad.reshape(local_grad.shape[1], -1), cells.T, preferred_element_type=jnp.float32
+    ).reshape(kernel.shape)
     grad_input = grad_extended[:, :, 1:]
     next_grad = from_behind(local_grad[:, :, :1], "space", -1)
     from_above = input_grad(next_grad, kernel, 2, 0)

time: 129 us -> 253 us (1.96)
  local copies, waits for them, and re-layouts: 22.6 us -> 151 us
  blocking collectives: 0 us -> 47.4 us
  waiting for transfers between devices: 45.8 us -> 19.2 us
  starting transfers between devices: 49 us -> 26.2 us
  matrix products: 9.64 us -> 3.63 us
  other arithmetic: 0.3 us -> 3.1 us
    slice x0 -> x27, local copies, waits for them, and re-layouts: none -> 137 us  [patches(): padded[:, a:a + planes:2, b:b + high:2, d:d + deep:2]]
    all_to_all x0 -> x1, blocking collectives: none -> 47.4 us  [summed_on_arrival(): lax.all_to_all(parts, axis, split_axis=0, concat_axis=0, tiled=True)]
    all_to_all x1 -> x0, waiting for transfers between devices: 24.9 us -> none  [summed_on_arrival(): lax.all_to_all(parts, axis, split_axis=0, concat_axis=0, tiled=True)]
    all_to_all x1 -> x0, starting transfers between devices: 24.4 us -> none  [summed_on_arrival(): lax.all_to_all(parts, axis, split_axis=0, concat_axis=0, tiled=True)]
    conv_general_dilated x2 -> x0, matrix products: 7.63 us -> none  [the longest x1 6.34 us: weight_grad(): lax.conv_general_dilated(inputs, grads, (1, 1, 1), [(0, 0), (1, 0), (1, 0...]
    concatenate x3 -> x0, local copies, waits for them, and re-layouts: 4.9 us -> none  [per_device(): extended = jnp.concatenate([below, volume], axis=2)]
    slice x4, local copies, waits for them, and re-layouts: 4.21 us -> 0.97 us  [per_device(): grad_input = grad_extended[:, :, 1:]]
    unnamed x14 -> x35, local copies, waits for them, and re-layouts: 7.32 us -> 6.82 us
  transfers between devices with their start and end apart: 5 -> 4, of which waited for: 4 -> 2; matrix products, arithmetic and copies ran while one was open for 11% -> 5% of each run, Pallas kernels for 0% -> 0%
where the time goes in v2:
time: 253 us; the launch traced here: 252 us
  local copies, waits for them, and re-layouts  151 us (60%)
  blocking collectives  47.4 us (19%)
  starting transfers between devices  26.2 us (10%)
  waiting for transfers between devices  19.2 us (8%)
  matrix products  3.63 us (1%)
  other arithmetic  3.1 us (1%)
    slice x27, local copies, waits for them, and re-layouts, patches(): padded[:, a:a + planes:2, b:b + high:2, d:d + deep:2]  137 us
    all_to_all x1, blocking collectives, summed_on_arrival(): lax.all_to_all(parts, axis, split_axis=0, concat_axis=0, tiled=True)  47.4 us
    all_to_all x2, waiting for transfers between devices, sent_to_all(): return lax.all_to_all(copies, axis, split_axis=0, concat_axis=0, tiled=True)  19.1 us
    ppermute x2, starting transfers between devices, from_behind(): return lax.ppermute(block, axis, route)  14.1 us
    all_to_all x2, starting transfers between devices, sent_to_all(): return lax.all_to_all(copies, axis, split_axis=0, concat_axis=0, tiled=True)  12.2 us
    unnamed x35, local copies, waits for them, and re-layouts  6.82 us
  transfers between devices with their start and end apart: 4, of which 2 were waited for; matrix products, arithmetic and copies ran while one was open for 5% of the time, Pallas kernels for 0%

profile of v2, /device:TPU:65, one launch (start us, length us, event | category | flops | bytes accessed | tf_op | source)
XLA Modules:
  0.0 252.2 jit_solution(1839960682021341110)
XLA Ops:
  0.6 0.9 slice.148
  1.6 11.2 %collective-permute-start = (bf16[1,32,1,16,128]{4,3,2,1,0:T(8,128)(2,1)S(1)}, bf16[1,32,1,16,128]{4,3,2,1,0:T(8,128)(2,1)S(1)}, u32[]{:S(2)}, u32[]{:S(2)}) collective-permute-start(bf16[1,32,1,16,128]{4,3,2,1,0:T(8,128)(2,1)S(1)} %slice.148), channel_id=1, source_target_pairs={{0,1},{1,2},{2,3},{3,4},{4,5},{5,6},{6,7},{7,8},{8,9},{9,10},{10,1... | collective-permute-start | bytes 393224 | tf_op jit(solution)/shard_map/ppermute | solution.py:10
  12.8 1.1 copy.307
  14.0 1.1 copy.314
  15.1 1.0 maximum_bitcast_fusion
  16.8 5.0 %slice.149 = bf16[32,1,8,64]{3,2,1,0:T(8,128)(2,1)S(1)} slice(bf16[32,3,17,129]{3,2,1,0:T(8,128)(2,1)S(1)} %pad.6), slice={[0:32:1], [0:1:1], [0:16:2], [0:128:2]} | slice | bytes 65536 | tf_op jit(solution)/shard_map/slice | solution.py:86
  21.8 5.0 %slice.150 = bf16[32,1,8,64]{3,2,1,0:T(8,128)(2,1)S(1)} slice(bf16[32,3,17,129]{3,2,1,0:T(8,128)(2,1)S(1)} %pad.6), slice={[0:32:1], [0:1:1], [0:16:2], [1:129:2]} | slice | bytes 65536 | tf_op jit(solution)/shard_map/slice | solution.py:86
  26.9 5.0 %slice.151 = bf16[32,1,8,64]{3,2,1,0:T(8,128)(2,1)S(1)} slice(bf16[32,3,17,129]{3,2,1,0:T(8,128)(2,1)S(1)} %pad.6), slice={[0:32:1], [0:1:1], [0:16:2], [2:129:2]} | slice | bytes 65536 | tf_op jit(solution)/shard_map/slice | solution.py:86
  31.9 5.0 %slice.152 = bf16[32,1,8,64]{3,2,1,0:T(8,128)(2,1)S(1)} slice(bf16[32,3,17,129]{3,2,1,0:T(8,128)(2,1)S(1)} %pad.6), slice={[0:32:1], [0:1:1], [1:17:2], [0:128:2]} | slice | bytes 65536 | tf_op jit(solution)/shard_map/slice | solution.py:86
  37.0 5.0 %slice.153 = bf16[32,1,8,64]{3,2,1,0:T(8,128)(2,1)S(1)} slice(bf16[32,3,17,129]{3,2,1,0:T(8,128)(2,1)S(1)} %pad.6), slice={[0:32:1], [0:1:1], [1:17:2], [1:129:2]} | slice | bytes 65536 | tf_op jit(solution)/shard_map/slice | solution.py:86
  42.0 5.0 %slice.154 = bf16[32,1,8,64]{3,2,1,0:T(8,128)(2,1)S(1)} slice(bf16[32,3,17,129]{3,2,1,0:T(8,128)(2,1)S(1)} %pad.6), slice={[0:32:1], [0:1:1], [1:17:2], [2:129:2]} | slice | bytes 65536 | tf_op jit(solution)/shard_map/slice | solution.py:86
  47.1 5.1 %slice.155 = bf16[32,1,8,64]{3,2,1,0:T(8,128)(2,1)S(1)} slice(bf16[32,3,17,129]{3,2,1,0:T(8,128)(2,1)S(1)} %pad.6), slice={[0:32:1], [0:1:1], [2:17:2], [0:128:2]} | slice | bytes 65536 | tf_op jit(solution)/shard_map/slice | solution.py:86
  52.2 5.1 %slice.156 = bf16[32,1,8,64]{3,2,1,0:T(8,128)(2,1)S(1)} slice(bf16[32,3,17,129]{3,2,1,0:T(8,128)(2,1)S(1)} %pad.6), slice={[0:32:1], [0:1:1], [2:17:2], [1:129:2]} | slice | bytes 65536 | tf_op jit(solution)/shard_map/slice | solution.py:86
  57.3 5.1 %slice.157 = bf16[32,1,8,64]{3,2,1,0:T(8,128)(2,1)S(1)} slice(bf16[32,3,17,129]{3,2,1,0:T(8,128)(2,1)S(1)} %pad.6), slice={[0:32:1], [0:1:1], [2:17:2], [2:129:2]} | slice | bytes 65536 | tf_op jit(solution)/shard_map/slice | solution.py:86
  62.4 5.0 %slice.158 = bf16[32,1,8,64]{3,2,1,0:T(8,128)(2,1)S(1)} slice(bf16[32,3,17,129]{3,2,1,0:T(8,128)(2,1)S(1)} %pad.6), slice={[0:32:1], [1:2:1], [0:16:2], [0:128:2]} | slice | bytes 65536 | tf_op jit(solution)/shard_map/slice | solution.py:86
  67.4 5.0 %slice.159 = bf16[32,1,8,64]{3,2,1,0:T(8,128)(2,1)S(1)} slice(bf16[32,3,17,129]{3,2,1,0:T(8,128)(2,1)S(1)} %pad.6), slice={[0:32:1], [1:2:1], [0:16:2], [1:129:2]} | slice | bytes 65536 | tf_op jit(solution)/shard_map/slice | solution.py:86
  72.5 5.0 %slice.160 = bf16[32,1,8,64]{3,2,1,0:T(8,128)(2,1)S(1)} slice(bf16[32,3,17,129]{3,2,1,0:T(8,128)(2,1)S(1)} %pad.6), slice={[0:32:1], [1:2:1], [0:16:2], [2:129:2]} | slice | bytes 65536 | tf_op jit(solution)/shard_map/slice | solution.py:86
  77.6 5.0 %slice.161 = bf16[32,1,8,64]{3,2,1,0:T(8,128)(2,1)S(1)} slice(bf16[32,3,17,129]{3,2,1,0:T(8,128)(2,1)S(1)} %pad.6), slice={[0:32:1], [1:2:1], [1:17:2], [0:128:2]} | slice | bytes 65536 | tf_op jit(solution)/shard_map/slice | solution.py:86
  82.6 5.0 %slice.162 = bf16[32,1,8,64]{3,2,1,0:T(8,128)(2,1)S(1)} slice(bf16[32,3,17,129]{3,2,1,0:T(8,128)(2,1)S(1)} %pad.6), slice={[0:32:1], [1:2:1], [1:17:2], [1:129:2]} | slice | bytes 65536 | tf_op jit(solution)/shard_map/slice | solution.py:86
  87.6 5.0 %slice.163 = bf16[32,1,8,64]{3,2,1,0:T(8,128)(2,1)S(1)} slice(bf16[32,3,17,129]{3,2,1,0:T(8,128)(2,1)S(1)} %pad.6), slice={[0:32:1], [1:2:1], [1:17:2], [2:129:2]} | slice | bytes 65536 | tf_op jit(solution)/shard_map/slice | solution.py:86
  92.7 5.1 %slice.164 = bf16[32,1,8,64]{3,2,1,0:T(8,128)(2,1)S(1)} slice(bf16[32,3,17,129]{3,2,1,0:T(8,128)(2,1)S(1)} %pad.6), slice={[0:32:1], [1:2:1], [2:17:2], [0:128:2]} | slice | bytes 65536 | tf_op jit(solution)/shard_map/slice | solution.py:86
  97.8 5.1 %slice.165 = bf16[32,1,8,64]{3,2,1,0:T(8,128)(2,1)S(1)} slice(bf16[32,3,17,129]{3,2,1,0:T(8,128)(2,1)S(1)} %pad.6), slice={[0:32:1], [1:2:1], [2:17:2], [1:129:2]} | slice | bytes 65536 | tf_op jit(solution)/shard_map/slice | solution.py:86
  102.9 5.1 %slice.166 = bf16[32,1,8,64]{3,2,1,0:T(8,128)(2,1)S(1)} slice(bf16[32,3,17,129]{3,2,1,0:T(8,128)(2,1)S(1)} %pad.6), slice={[0:32:1], [1:2:1], [2:17:2], [2:129:2]} | slice | bytes 65536 | tf_op jit(solution)/shard_map/slice | solution.py:86
  108.0 5.0 %slice.167 = bf16[32,1,8,64]{3,2,1,0:T(8,128)(2,1)S(1)} slice(bf16[32,3,17,129]{3,2,1,0:T(8,128)(2,1)S(1)} %pad.6), slice={[0:32:1], [2:3:1], [0:16:2], [0:128:2]} | slice | bytes 65536 | tf_op jit(solution)/shard_map/slice | solution.py:86
  113.0 5.0 %slice.168 = bf16[32,1,8,64]{3,2,1,0:T(8,128)(2,1)S(1)} slice(bf16[32,3,17,129]{3,2,1,0:T(8,128)(2,1)S(1)} %pad.6), slice={[0:32:1], [2:3:1], [0:16:2], [1:129:2]} | slice | bytes 65536 | tf_op jit(solution)/shard_map/slice | solution.py:86
  118.1 5.0 %slice.169 = bf16[32,1,8,64]{3,2,1,0:T(8,128)(2,1)S(1)} slice(bf16[32,3,17,129]{3,2,1,0:T(8,128)(2,1)S(1)} %pad.6), slice={[0:32:1], [2:3:1], [0:16:2], [2:129:2]} | slice | bytes 65536 | tf_op jit(solution)/shard_map/slice | solution.py:86
  123.2 5.0 %slice.170 = bf16[32,1,8,64]{3,2,1,0:T(8,128)(2,1)S(1)} slice(bf16[32,3,17,129]{3,2,1,0:T(8,128)(2,1)S(1)} %pad.6), slice={[0:32:1], [2:3:1], [1:17:2], [0:128:2]} | slice | bytes 65536 | tf_op jit(solution)/shard_map/slice | solution.py:86
  128.2 5.0 %slice.171 = bf16[32,1,8,64]{3,2,1,0:T(8,128)(2,1)S(1)} slice(bf16[32,3,17,129]{3,2,1,0:T(8,128)(2,1)S(1)} %pad.6), slice={[0:32:1], [2:3:1], [1:17:2], [1:129:2]} | slice | bytes 65536 | tf_op jit(solution)/shard_map/slice | solution.py:86
  133.3 5.0 %slice.172 = bf16[32,1,8,64]{3,2,1,0:T(8,128)(2,1)S(1)} slice(bf16[32,3,17,129]{3,2,1,0:T(8,128)(2,1)S(1)} %pad.6), slice={[0:32:1], [2:3:1], [1:17:2], [2:129:2]} | slice | bytes 65536 | tf_op jit(solution)/shard_map/slice | solution.py:86
  138.3 5.1 %slice.173 = bf16[32,1,8,64]{3,2,1,0:T(8,128)(2,1)S(1)} slice(bf16[32,3,17,129]{3,2,1,0:T(8,128)(2,1)S(1)} %pad.6), slice={[0:32:1], [2:3:1], [2:17:2], [0:128:2]} | slice | bytes 65536 | tf_op jit(solution)/shard_map/slice | solution.py:86
  143.4 5.1 %slice.174 = bf16[32,1,8,64]{3,2,1,0:T(8,128)(2,1)S(1)} slice(bf16[32,3,17,129]{3,2,1,0:T(8,128)(2,1)S(1)} %pad.6), slice={[0:32:1], [2:3:1], [2:17:2], [1:129:2]} | slice | bytes 65536 | tf_op jit(solution)/shard_map/slice | solution.py:86
  148.5 5.1 %slice.175 = bf16[32,1,8,64]{3,2,1,0:T(8,128)(2,1)S(1)} slice(bf16[32,3,17,129]{3,2,1,0:T(8,128)(2,1)S(1)} %pad.6), slice={[0:32:1], [2:3:1], [2:17:2], [2:129:2]} | slice | bytes 65536 | tf_op jit(solution)/shard_map/slice | solution.py:86
  154.4 1.1 reshape.192
  156.1 0.9 multiply_convert_fusion
  158.0 47.4 %all_to_all.21 = f32[64,1,864]{2,1,0:T(1,128)S(1)} all-to-all(f32[64,1,864]{2,1,0:T(1,128)S(1)} %copy.324), channel_id=1, replica_groups=mesh['dp'=16,'space'=64] {'space'}, dimensions={0} | all-to-all | bytes 442368 | tf_op jit(solution)/shard_map/all_to_all | solution.py:21
  206.2 5.6 %all-to-all-start.1 = ((f32[16,1,864]{2,1,0:T(1,128)}), f32[16,1,864]{2,1,0:T(1,128)S(1)}, u32[]{:S(2)}, u32[]{:S(2)}) async-start(f32[16,1,864]{2,1,0:T(1,128)} %broadcast_in_dim.6), calls=%async_computation.1 | async-start | bytes 114688 | tf_op jit(solution)/shard_map/all_to_all | solution.py:27
  211.8 2.9 %collective-permute-start.1 = (bf16[1,64,1,8,64]{1,3,4,2,0:T(8,128)(2,1)S(1)}, bf16[1,64,1,8,64]{1,3,4,2,0:T(8,128)(2,1)}, u32[]{:S(2)}, u32[]{:S(2)}) collective-permute-start(bf16[1,64,1,8,64]{1,3,4,2,0:T(8,128)(2,1)S(1)} %get-tuple-element.33), channel_id=1, source_target_pairs={{1,0},{2,1},{3,2},{4,3},{5,4},{6,5},{7,6},{8,7},{9,8},{10,9},{11,1... | collective-permute-start | bytes 196616 | tf_op jit(solution)/shard_map/ppermute | solution.py:10
  214.8 2.8 %all-to-all-done.1 = f32[16,1,864]{2,1,0:T(1,128)S(1)} async-done(((f32[16,1,864]{2,1,0:T(1,128)}), f32[16,1,864]{2,1,0:T(1,128)S(1)}, u32[]{:S(2)}, u32[]{:S(2)}) %all-to-all-start.1) | async-done | bytes 55328 | tf_op jit(solution)/shard_map/all_to_all | solution.py:27
  217.6 0.8 broadcast_in_dim.7
  218.4 6.6 %all-to-all-start.2 = ((f32[64,1,864]{2,1,0:T(1,128)}), f32[64,1,864]{2,1,0:T(1,128)}, u32[]{:S(2)}, u32[]{:S(2)}) async-start(f32[64,1,864]{2,1,0:T(1,128)} %broadcast_in_dim.7), calls=%async_computation.2 | async-start | bytes 458752 | tf_op jit(solution)/shard_map/all_to_all | solution.py:27
  225.1 1.2 convolution_select_fusion
  227.2 1.7 copy.328
  228.9 0.9 pad.9
  229.9 1.8 fusion
  231.9 1.7 copy.329
  233.6 16.3 %all-to-all-done.2 = f32[64,1,864]{2,1,0:T(1,128)} async-done(((f32[64,1,864]{2,1,0:T(1,128)}), f32[64,1,864]{2,1,0:T(1,128)}, u32[]{:S(2)}, u32[]{:S(2)}) %all-to-all-start.2) | async-done | bytes 221216 | tf_op jit(solution)/shard_map/all_to_all | solution.py:27
  250.0 1.0 copy_multiply_fusion
  251.3 0.8 copy.330
  (57 shorter events, 5.6 us)
Async XLA Ops:
  1.6 13.6 %collective-permute-start = (bf16[1,32,1,16,128]{4,3,2,1,0:T(8,128)(2,1)S(1)}, bf16[1,32,1,16,128]{4,3,2,1,0:T(8,128)(2,1)S(1)}, u32[]{:S(2)}, u32[]{:S(2)}) collective-permute-start(bf16[1,32,1,16,128]{4,3,2,1,0:T(8,128)(2,1)S(1)} %slice.148), channel_id=1, source_target_pairs={{0,1},{1,2},{2,3},{3,4},{4,5},{5,6},{6,7},{7,8},{8,9},{9,10},{10,1... | collective-permute-start | bytes 393224 | tf_op jit(solution)/shard_map/ppermute | solution.py:10
  157.3 67.7 %copy-start.1 = (pred[8,18]{0,1:T(8,128)(4,1)S(1)}, pred[8,18]{0,1:T(8,128)(4,1)}, u32[]{:S(2)}) copy-start(pred[8,18]{0,1:T(8,128)(4,1)} %constant.57) | copy-start | bytes 436
  157.8 67.3 %copy-start = (bf16[64,32,3,3,3]{0,1,4,3,2:T(8,128)(2,1)S(1)}, bf16[64,32,3,3,3]{0,1,4,3,2:T(8,128)(2,1)}, u32[]{:S(2)}) copy-start(bf16[64,32,3,3,3]{0,1,4,3,2:T(8,128)(2,1)} %param.6) | copy-start | bytes 331780
  206.2 11.3 %all-to-all-start.1 = ((f32[16,1,864]{2,1,0:T(1,128)}), f32[16,1,864]{2,1,0:T(1,128)S(1)}, u32[]{:S(2)}, u32[]{:S(2)}) async-start(f32[16,1,864]{2,1,0:T(1,128)} %broadcast_in_dim.6), calls=%async_computation.1 | async-start | bytes 114688 | tf_op jit(solution)/shard_map/all_to_all | solution.py:27
  211.8 17.1 %collective-permute-start.1 = (bf16[1,64,1,8,64]{1,3,4,2,0:T(8,128)(2,1)S(1)}, bf16[1,64,1,8,64]{1,3,4,2,0:T(8,128)(2,1)}, u32[]{:S(2)}, u32[]{:S(2)}) collective-permute-start(bf16[1,64,1,8,64]{1,3,4,2,0:T(8,128)(2,1)S(1)} %get-tuple-element.33), channel_id=1, source_target_pairs={{1,0},{2,1},{3,2},{4,3},{5,4},{6,5},{7,6},{8,7},{9,8},{10,9},{11,1... | collective-permute-start | bytes 196616 | tf_op jit(solution)/shard_map/ppermute | solution.py:10
  218.4 31.6 %all-to-all-start.2 = ((f32[64,1,864]{2,1,0:T(1,128)}), f32[64,1,864]{2,1,0:T(1,128)}, u32[]{:S(2)}, u32[]{:S(2)}) async-start(f32[64,1,864]{2,1,0:T(1,128)} %broadcast_in_dim.7), calls=%async_computation.2 | async-start | bytes 458752 | tf_op jit(solution)/shard_map/all_to_all | solution.py:27

commit v3 on v2

--- a/solution.py
+++ b/solution.py
@@ -81,16 +81,18 @@
 
 def patches(extended):
     planes, high, deep = extended.shape[2] - 1, extended.shape[3], extended.shape[4]
-    padded = jnp.pad(extended[0], ((0, 0), (0, 0), (1, 0), (1, 0)))
+    channels = extended.shape[1]
+    padded = jnp.pad(extended[0], ((0, 0), (0, 0), (1, 1), (1, 1)))
+    split = padded.reshape(channels, planes + 1, high // 2 + 1, 2, deep // 2 + 1, 2)
+    split = jnp.transpose(split, (0, 1, 3, 5, 2, 4))
     taps = [
-        padded[:, a : a + planes : 2, b : b + high : 2, d : d + deep : 2]
+        split[:, a : a + planes : 2, b % 2, d % 2, b // 2 : b // 2 + high // 2, d // 2 : d // 2 + deep // 2]
         for a in range(3)
         for b in range(3)
         for d in range(3)
     ]
     cells = jnp.stack(taps, axis=1)
-    return cells.reshape(cells.shape[0] * 27, -1)
-
+    return cells.reshape(channels * 27, -1)
 
 def per_device(volume, kernel, cotangent):
     below = from_behind(volume[:, :, -1:], "space", 1)

time: 253 us -> 175 us (0.69)
  local copies, waits for them, and re-layouts: 151 us -> 69 us
  blocking collectives: 47.4 us -> 0 us
  starting transfers between devices: 26.2 us -> 52.4 us
  waiting for transfers between devices: 19.2 us -> 44.2 us
    slice x27 -> x29, local copies, waits for them, and re-layouts: 137 us -> 28.6 us  [patches(): split[:, a:a + planes:2, b % 2, d % 2, b // 2:b // 2 + high // 2, d // 2:...]
    all_to_all x1 -> x0, blocking collectives: 47.4 us -> none  [summed_on_arrival(): lax.all_to_all(parts, axis, split_axis=0, concat_axis=0, tiled=True)]
    all_to_all x0 -> x1, starting transfers between devices: none -> 24.4 us  [summed_on_arrival(): lax.all_to_all(parts, axis, split_axis=0, concat_axis=0, tiled=True)]
    all_to_all x0 -> x1, waiting for transfers between devices: none -> 21.1 us  [summed_on_arrival(): lax.all_to_all(parts, axis, split_axis=0, concat_axis=0, tiled=True)]
    unnamed x35 -> x80, local copies, waits for them, and re-layouts: 6.82 us -> 21.1 us
    reshape x1 -> x2, local copies, waits for them, and re-layouts: 1.08 us -> 4.96 us  [the longest x1 3.88 us: patches(): padded.reshape(channels, planes + 1, high // 2 + 1, 2, deep // 2 + 1, 2)]
    all_to_all x2, waiting for transfers between devices: 19.1 us -> 22.6 us  [sent_to_all(): return lax.all_to_all(copies, axis, split_axis=0, concat_axis=0, tiled=True)]
  transfers between devices with their start and end apart: 4 -> 5, of which waited for: 2 -> 4; matrix products, arithmetic and copies ran while one was open for 5% -> 8% of each run, Pallas kernels for 0% -> 0%
where the time goes in v3:
time: 175 us; the launch traced here: 174 us
  local copies, waits for them, and re-layouts  69 us (39%)
  starting transfers between devices  52.4 us (30%)
  waiting for transfers between devices  44.2 us (25%)
  other arithmetic  4.02 us (2%)
  matrix products  3.71 us (2%)
    slice x29, local copies, waits for them, and re-layouts, patches(): split[:, a:a + planes:2, b % 2, d % 2, b // 2:b // 2 + high // 2, d // 2:...  28.6 us
    all_to_all x1, starting transfers between devices, summed_on_arrival(): lax.all_to_all(parts, axis, split_axis=0, concat_axis=0, tiled=True)  24.4 us
    all_to_all x2, waiting for transfers between devices, sent_to_all(): return lax.all_to_all(copies, axis, split_axis=0, concat_axis=0, tiled=True)  22.6 us
    all_to_all x1, waiting for transfers between devices, summed_on_arrival(): lax.all_to_all(parts, axis, split_axis=0, concat_axis=0, tiled=True)  21.1 us
    unnamed x80, local copies, waits for them, and re-layouts  21.1 us
    all_to_all x2, starting transfers between devices, sent_to_all(): return lax.all_to_all(copies, axis, split_axis=0, concat_axis=0, tiled=True)  14.5 us
    ppermute x2, starting transfers between devices, from_behind(): return lax.ppermute(block, axis, route)  13.6 us
    reshape x1, local copies, waits for them, and re-layouts, patches(): padded.reshape(channels, planes + 1, high // 2 + 1, 2, deep // 2 + 1, 2)  3.88 us
  transfers between devices with their start and end apart: 5, of which 4 were waited for; matrix products, arithmetic and copies ran while one was open for 8% of the time, Pallas kernels for 0%

profile of v3, /device:TPU:65, one launch (start us, length us, event | category | flops | bytes accessed | tf_op | source)
XLA Modules:
  0.0 174.5 jit_solution(7664632252914959879)
XLA Ops:
  0.6 0.9 slice.148
  1.6 11.2 %collective-permute-start = (bf16[1,32,1,16,128]{4,3,2,1,0:T(8,128)(2,1)S(1)}, bf16[1,32,1,16,128]{4,3,2,1,0:T(8,128)(2,1)S(1)}, u32[]{:S(2)}, u32[]{:S(2)}) collective-permute-start(bf16[1,32,1,16,128]{4,3,2,1,0:T(8,128)(2,1)S(1)} %slice.148), channel_id=1, source_target_pairs={{0,1},{1,2},{2,3},{3,4},{4,5},{5,6},{6,7},{7,8},{8,9},{9,10},{10,1... | collective-permute-start | bytes 393224 | tf_op jit(solution)/shard_map/ppermute | solution.py:10
  12.8 1.1 copy.1869
  13.9 0.8 reshape.197
  15.1 1.0 maximum_bitcast_fusion
  16.1 0.9 copy.1886
  17.1 1.8 %pad.6.clone = bf16[32,3,18,130]{0,3,2,1:T(8,128)(2,1)} pad(bf16[32,3,16,128]{0,3,2,1:T(8,128)(2,1)S(1)} %copy.1886, bf16[]{:T(256)} %constant.37.clone.1), padding=0_0x0_0x1_1x1_1 | pad | bytes 842498 | tf_op jit(solution)/shard_map/jit(_pad)/pad | solution.py:85
  18.9 3.9 %reshape.195 = bf16[32,3,9,2,65,2]{0,5,4,3,2,1:T(2,128)(2,1)S(1)} reshape(bf16[32,3,18,130]{0,3,2,1:T(8,128)(2,1)} %pad.6.clone) | data formatting | bytes 898560 | tf_op jit(solution)/shard_map/reshape | solution.py:86
  22.8 2.9 %fusion.15 = (bf16[32,1,1,1,8,64]{0,3,5,2,4,1:T(2,128)(2,1)}, bf16[32,1,1,1,8,64]{0,3,5,2,4,1:T(2,128)(2,1)}, bf16[32,1,1,1,8,64]{0,3,5,2,4,1:T(2,128)(2,1)}, bf...) fusion(bf16[32,3,2,2,9,65]{0,3,5,2,4,1:T(2,128)(2,1)S(1)} %bitc, ...), kind=kLoop, calls=%fused_computation.53 | loop fusion | bytes 524288 | tf_op jit(solution)/shard_map/slice | solution.py:89
  25.7 5.0 %fusion.14 = (bf16[32,1,1,1,8,64]{0,3,5,2,4,1:T(2,128)(2,1)S(1)}, bf16[32,1,1,1,8,64]{0,3,5,2,4,1:T(2,128)(2,1)S(1)}, bf16[32,1,1,1,8,64]{0,3,5,2,4,1:T(2,128)(2...) fusion(bf16[32,3,2,2,9,65]{0,3,5,2,4,1:T(2,128)(2,1)S(1)} %bitc, ...), kind=kLoop, calls=%fused_computation.52 | loop fusion | bytes 1245184 | tf_op jit(solution)/shard_map/slice | solution.py:89
  30.7 1.2 copy.1841
  32.5 1.7 copy.1842
  34.2 1.7 copy.1843
  35.9 1.7 copy.1844
  37.7 1.8 %copy.1845 = bf16[32,1,1,1,8,64]{5,4,0,3,2,1:T(8,128)(2,1)} copy(bf16[32,1,1,1,8,64]{0,3,5,2,4,1:T(2,128)(2,1)} %get-tuple-element.130) | data formatting | bytes 65536 | tf_op jit(solution)/shard_map/slice | solution.py:89
  39.5 0.8 copy.1846
  40.2 0.8 copy.1847
  41.0 0.8 copy.1848
  41.8 0.8 copy.1849
  42.5 1.8 %copy.1850 = bf16[32,1,1,1,8,64]{5,4,0,3,2,1:T(8,128)(2,1)} copy(bf16[32,1,1,1,8,64]{0,3,5,2,4,1:T(2,128)(2,1)} %get-tuple-element.125) | data formatting | bytes 65536 | tf_op jit(solution)/shard_map/slice | solution.py:89
  44.3 1.7 copy.1851
  46.0 1.1 copy.1852
  47.1 1.1 copy.1853
  48.2 1.1 copy.1854
  49.3 1.1 copy.1855
  68.8 1.8 %copy.1868 = bf16[32,27,1,8,64]{4,3,1,0,2:T(8,128)(2,1)S(1)} copy(bf16[32,27,1,8,64]{4,3,0,2,1:T(8,128)(2,1)} %bitcast_dynamic-update-slice_fusion) | data formatting | bytes 1769472 | tf_op jit(solution)/shard_map/stack | solution.py:94
  70.6 1.1 reshape.196
  72.1 1.0 multiply_convert_fusion
  73.1 1.1 reshape.199
  74.6 0.9 copy.1878
  75.5 24.4 %all-to-all-start = ((f32[64,1,864]{2,1,0:T(1,128)}), f32[64,1,864]{2,1,0:T(1,128)S(1)}, u32[]{:S(2)}, u32[]{:S(2)}) async-start(f32[64,1,864]{2,1,0:T(1,128)} %copy.1878), calls=%async_computation | async-start | bytes 458752 | tf_op jit(solution)/shard_map/all_to_all | solution.py:21
  99.9 2.4 %collective-permute-start.1 = (bf16[1,64,1,8,64]{4,3,1,2,0:T(8,128)(2,1)}, bf16[1,64,1,8,64]{4,3,1,2,0:T(8,128)(2,1)}, u32[]{:S(2)}, u32[]{:S(2)}) collective-permute-start(bf16[1,64,1,8,64]{4,3,1,2,0:T(8,128)(2,1)} %get-tuple-element.135), channel_id=1, source_target_pairs={{1,0},{2,1},{3,2},{4,3},{5,4},{6,5},{7,6},{8,7},{9,8},{10,9},{11,1... | collective-permute-start | bytes 196616 | tf_op jit(solution)/shard_map/ppermute | solution.py:10
  102.3 1.1 copy.1871
  103.4 21.1 %all-to-all-done = f32[64,1,864]{2,1,0:T(1,128)S(1)} async-done(((f32[64,1,864]{2,1,0:T(1,128)}), f32[64,1,864]{2,1,0:T(1,128)S(1)}, u32[]{:S(2)}, u32[]{:S(2)}) %all-to-all-start) | async-done | bytes 221216 | tf_op jit(solution)/shard_map/all_to_all | solution.py:21
  125.4 5.2 %all-to-all-start.1 = ((f32[16,1,864]{2,1,0:T(1,128)}), f32[16,1,864]{2,1,0:T(1,128)}, u32[]{:S(2)}, u32[]{:S(2)}) async-start(f32[16,1,864]{2,1,0:T(1,128)} %broadcast_in_dim.6), calls=%async_computation.1 | async-start | bytes 114688 | tf_op jit(solution)/shard_map/all_to_all | solution.py:27
  130.6 1.2 convolution_select_fusion
  131.8 0.8 copy.1873
  132.6 3.9 %all-to-all-done.1 = f32[16,1,864]{2,1,0:T(1,128)} async-done(((f32[16,1,864]{2,1,0:T(1,128)}), f32[16,1,864]{2,1,0:T(1,128)}, u32[]{:S(2)}, u32[]{:S(2)}) %all-to-all-start.1) | async-done | bytes 55328 | tf_op jit(solution)/shard_map/all_to_all | solution.py:27
  136.4 0.9 reduce_sum.19
  137.3 0.8 broadcast_in_dim.7
  138.1 9.3 %all-to-all-start.2 = ((f32[64,1,864]{2,1,0:T(1,128)}), f32[64,1,864]{2,1,0:T(1,128)}, u32[]{:S(2)}, u32[]{:S(2)}) async-start(f32[64,1,864]{2,1,0:T(1,128)} %broadcast_in_dim.7), calls=%async_computation.2 | async-start | bytes 458752 | tf_op jit(solution)/shard_map/all_to_all | solution.py:27
  147.4 1.2 slice_bitcast_fusion
  148.5 1.1 copy.1874
  149.7 1.8 %fusion = bf16[1,16,8,18,32]{4,2,3,1,0:T(8,128)(2,1)S(1)} fusion(bf16[64,32,3,3,3]{0,1,4,3,2:T(8,128)(2,1)} %param.6, f32[2,16,8,18,32]{4,2,3,1,0:T(8,128)S(1)} %convolution_select_fusion, pred[8,18]{0,1:T(8,128)(4,1)S(1)} %copy-done.24, bf16[64,1,8,1,8,10]{0,2,5,4,3,1:T(8,128)(2,1)S(1)} %fusion.8), kind=kOutput, calls=%fused_computation.3 | convolution fusion | flops 20570112 | bytes 635024 | tf_op jit(solution)/shard_map/conv_general_dilated | solution.py:59
  151.8 1.7 copy.1883
  153.6 18.8 %all-to-all-done.2 = f32[64,1,864]{2,1,0:T(1,128)} async-done(((f32[64,1,864]{2,1,0:T(1,128)}), f32[64,1,864]{2,1,0:T(1,128)}, u32[]{:S(2)}, u32[]{:S(2)}) %all-to-all-start.2) | async-done | bytes 221216 | tf_op jit(solution)/shard_map/all_to_all | solution.py:27
  172.3 1.0 copy_multiply_fusion
  173.7 0.8 copy.1884
  (106 shorter events, 21.6 us)
Async XLA Ops:
  1.6 13.6 %collective-permute-start = (bf16[1,32,1,16,128]{4,3,2,1,0:T(8,128)(2,1)S(1)}, bf16[1,32,1,16,128]{4,3,2,1,0:T(8,128)(2,1)S(1)}, u32[]{:S(2)}, u32[]{:S(2)}) collective-permute-start(bf16[1,32,1,16,128]{4,3,2,1,0:T(8,128)(2,1)S(1)} %slice.148), channel_id=1, source_target_pairs={{0,1},{1,2},{2,3},{3,4},{4,5},{5,6},{6,7},{7,8},{8,9},{9,10},{10,1... | collective-permute-start | bytes 393224 | tf_op jit(solution)/shard_map/ppermute | solution.py:10
  30.6 8.8 %copy-start.11 = (bf16[32,1,1,1,8,64]{0,3,5,2,4,1:T(2,128)(2,1)S(1)}, bf16[32,1,1,1,8,64]{0,3,5,2,4,1:T(2,128)(2,1)}, u32[]{:S(2)}) copy-start(bf16[32,1,1,1,8,64]{0,3,5,2,4,1:T(2,128)(2,1)} %get-tuple-element.129) | copy-start | bytes 98308
  30.6 9.6 %copy-start.10 = (bf16[32,1,1,1,8,64]{0,3,5,2,4,1:T(2,128)(2,1)S(1)}, bf16[32,1,1,1,8,64]{0,3,5,2,4,1:T(2,128)(2,1)}, u32[]{:S(2)}) copy-start(bf16[32,1,1,1,8,64]{0,3,5,2,4,1:T(2,128)(2,1)} %get-tuple-element.128) | copy-start | bytes 98308
  30.6 10.3 %copy-start.9 = (bf16[32,1,1,1,8,64]{0,3,5,2,4,1:T(2,128)(2,1)S(1)}, bf16[32,1,1,1,8,64]{0,3,5,2,4,1:T(2,128)(2,1)}, u32[]{:S(2)}) copy-start(bf16[32,1,1,1,8,64]{0,3,5,2,4,1:T(2,128)(2,1)} %get-tuple-element.127) | copy-start | bytes 98308
  30.7 11.1 %copy-start.8 = (bf16[32,1,1,1,8,64]{0,3,5,2,4,1:T(2,128)(2,1)S(1)}, bf16[32,1,1,1,8,64]{0,3,5,2,4,1:T(2,128)(2,1)}, u32[]{:S(2)}) copy-start(bf16[32,1,1,1,8,64]{0,3,5,2,4,1:T(2,128)(2,1)} %get-tuple-element.126) | copy-start | bytes 98308
  37.7 12.8 %copy-start.7 = (bf16[32,1,1,1,8,64]{0,3,5,2,4,1:T(2,128)(2,1)S(1)}, bf16[32,1,1,1,8,64]{0,3,5,2,4,1:T(2,128)(2,1)}, u32[]{:S(2)}) copy-start(bf16[32,1,1,1,8,64]{0,3,5,2,4,1:T(2,128)(2,1)} %get-tuple-element.119) | copy-start | bytes 98308
  39.5 11.1 %copy-start.6 = (bf16[32,1,1,1,8,64]{0,3,5,2,4,1:T(2,128)(2,1)S(1)}, bf16[32,1,1,1,8,64]{0,3,5,2,4,1:T(2,128)(2,1)}, u32[]{:S(2)}) copy-start(bf16[32,1,1,1,8,64]{0,3,5,2,4,1:T(2,128)(2,1)} %get-tuple-element.118) | copy-start | bytes 98308
  40.2 10.6 %copy-start.5 = (bf16[32,1,1,1,8,64]{0,3,5,2,4,1:T(2,128)(2,1)S(1)}, bf16[32,1,1,1,8,64]{0,3,5,2,4,1:T(2,128)(2,1)}, u32[]{:S(2)}) copy-start(bf16[32,1,1,1,8,64]{0,3,5,2,4,1:T(2,128)(2,1)} %get-tuple-element.117) | copy-start | bytes 98308
  41.0 10.0 %copy-start.4 = (bf16[32,1,1,1,8,64]{0,3,5,2,4,1:T(2,128)(2,1)S(1)}, bf16[32,1,1,1,8,64]{0,3,5,2,4,1:T(2,128)(2,1)}, u32[]{:S(2)}) copy-start(bf16[32,1,1,1,8,64]{0,3,5,2,4,1:T(2,128)(2,1)} %get-tuple-element.116) | copy-start | bytes 98308
  41.8 9.4 %copy-start.3 = (bf16[32,1,1,1,8,64]{0,3,5,2,4,1:T(2,128)(2,1)S(1)}, bf16[32,1,1,1,8,64]{0,3,5,2,4,1:T(2,128)(2,1)}, u32[]{:S(2)}) copy-start(bf16[32,1,1,1,8,64]{0,3,5,2,4,1:T(2,128)(2,1)} %get-tuple-element.115) | copy-start | bytes 98308
  42.5 8.8 %copy-start.2 = (bf16[32,1,1,1,8,64]{0,3,5,2,4,1:T(2,128)(2,1)S(1)}, bf16[32,1,1,1,8,64]{0,3,5,2,4,1:T(2,128)(2,1)}, u32[]{:S(2)}) copy-start(bf16[32,1,1,1,8,64]{0,3,5,2,4,1:T(2,128)(2,1)} %get-tuple-element.114) | copy-start | bytes 98308
  50.6 1.8 %copy-start.21 = (bf16[32,1,1,1,8,64]{5,4,0,3,2,1:T(8,128)(2,1)S(1)}, bf16[32,1,1,1,8,64]{5,4,0,3,2,1:T(8,128)(2,1)}, u32[]{:S(2)}) copy-start(bf16[32,1,1,1,8,64]{5,4,0,3,2,1:T(8,128)(2,1)} %copy.1842) | copy-start | bytes 98308
  50.8 2.2 %copy-start.22 = (bf16[32,1,1,1,8,64]{5,4,0,3,2,1:T(8,128)(2,1)S(1)}, bf16[32,1,1,1,8,64]{5,4,0,3,2,1:T(8,128)(2,1)}, u32[]{:S(2)}) copy-start(bf16[32,1,1,1,8,64]{5,4,0,3,2,1:T(8,128)(2,1)} %copy.1843) | copy-start | bytes 98308
  50.8 2.9 %copy-start.20 = (bf16[32,1,1,1,8,64]{5,4,0,3,2,1:T(8,128)(2,1)S(1)}, bf16[32,1,1,1,8,64]{5,4,0,3,2,1:T(8,128)(2,1)}, u32[]{:S(2)}) copy-start(bf16[32,1,1,1,8,64]{5,4,0,3,2,1:T(8,128)(2,1)} %copy.1844) | copy-start | bytes 98308
  50.8 3.5 %copy-start.19 = (bf16[32,1,1,1,8,64]{5,4,0,3,2,1:T(8,128)(2,1)S(1)}, bf16[32,1,1,1,8,64]{5,4,0,3,2,1:T(8,128)(2,1)}, u32[]{:S(2)}) copy-start(bf16[32,1,1,1,8,64]{5,4,0,3,2,1:T(8,128)(2,1)} %copy.1845) | copy-start | bytes 98308
  51.0 3.9 %copy-start.18 = (bf16[32,1,1,1,8,64]{5,4,0,3,2,1:T(8,128)(2,1)S(1)}, bf16[32,1,1,1,8,64]{5,4,0,3,2,1:T(8,128)(2,1)}, u32[]{:S(2)}) copy-start(bf16[32,1,1,1,8,64]{5,4,0,3,2,1:T(8,128)(2,1)} %copy.1846) | copy-start | bytes 98308
  51.0 4.6 %copy-start.16 = (bf16[32,1,1,1,8,64]{5,4,0,3,2,1:T(8,128)(2,1)S(1)}, bf16[32,1,1,1,8,64]{5,4,0,3,2,1:T(8,128)(2,1)}, u32[]{:S(2)}) copy-start(bf16[32,1,1,1,8,64]{5,4,0,3,2,1:T(8,128)(2,1)} %copy.1847) | copy-start | bytes 98308
  51.1 5.0 %copy-start.17 = (bf16[32,1,1,1,8,64]{5,4,0,3,2,1:T(8,128)(2,1)S(1)}, bf16[32,1,1,1,8,64]{5,4,0,3,2,1:T(8,128)(2,1)}, u32[]{:S(2)}) copy-start(bf16[32,1,1,1,8,64]{5,4,0,3,2,1:T(8,128)(2,1)} %copy.1848) | copy-start | bytes 98308
  51.2 5.7 %copy-start.15 = (bf16[32,1,1,1,8,64]{5,4,0,3,2,1:T(8,128)(2,1)S(1)}, bf16[32,1,1,1,8,64]{5,4,0,3,2,1:T(8,128)(2,1)}, u32[]{:S(2)}) copy-start(bf16[32,1,1,1,8,64]{5,4,0,3,2,1:T(8,128)(2,1)} %copy.1849) | copy-start | bytes 98308
  51.2 6.3 %copy-start.14 = (bf16[32,1,1,1,8,64]{5,4,0,3,2,1:T(8,128)(2,1)S(1)}, bf16[32,1,1,1,8,64]{5,4,0,3,2,1:T(8,128)(2,1)}, u32[]{:S(2)}) copy-start(bf16[32,1,1,1,8,64]{5,4,0,3,2,1:T(8,128)(2,1)} %copy.1850) | copy-start | bytes 98308
  51.3 6.7 %copy-start.13 = (bf16[32,1,1,1,8,64]{5,4,0,3,2,1:T(8,128)(2,1)S(1)}, bf16[32,1,1,1,8,64]{5,4,0,3,2,1:T(8,128)(2,1)}, u32[]{:S(2)}) copy-start(bf16[32,1,1,1,8,64]{5,4,0,3,2,1:T(8,128)(2,1)} %copy.1851) | copy-start | bytes 98308
  70.6 1.1 copy-start.12
  70.6 1.5 copy-start.23
  73.1 57.5 %copy-start.1 = (bf16[64,32,3,3,3]{0,1,4,3,2:T(8,128)(2,1)S(1)}, bf16[64,32,3,3,3]{0,1,4,3,2:T(8,128)(2,1)}, u32[]{:S(2)}) copy-start(bf16[64,32,3,3,3]{0,1,4,3,2:T(8,128)(2,1)} %param.6) | copy-start | bytes 331780
  73.1 57.5 %copy-start.24 = (pred[8,18]{0,1:T(8,128)(4,1)S(1)}, pred[8,18]{0,1:T(8,128)(4,1)}, u32[]{:S(2)}) copy-start(pred[8,18]{0,1:T(8,128)(4,1)} %constant.57) | copy-start | bytes 436
  75.5 49.1 %all-to-all-start = ((f32[64,1,864]{2,1,0:T(1,128)}), f32[64,1,864]{2,1,0:T(1,128)S(1)}, u32[]{:S(2)}, u32[]{:S(2)}) async-start(f32[64,1,864]{2,1,0:T(1,128)} %copy.1878), calls=%async_computation | async-start | bytes 458752 | tf_op jit(solution)/shard_map/all_to_all | solution.py:21
  99.9 48.6 %collective-permute-start.1 = (bf16[1,64,1,8,64]{4,3,1,2,0:T(8,128)(2,1)}, bf16[1,64,1,8,64]{4,3,1,2,0:T(8,128)(2,1)}, u32[]{:S(2)}, u32[]{:S(2)}) collective-permute-start(bf16[1,64,1,8,64]{4,3,1,2,0:T(8,128)(2,1)} %get-tuple-element.135), channel_id=1, source_target_pairs={{1,0},{2,1},{3,2},{4,3},{5,4},{6,5},{7,6},{8,7},{9,8},{10,9},{11,1... | collective-permute-start | bytes 196616 | tf_op jit(solution)/shard_map/ppermute | solution.py:10
  125.4 11.0 %all-to-all-start.1 = ((f32[16,1,864]{2,1,0:T(1,128)}), f32[16,1,864]{2,1,0:T(1,128)}, u32[]{:S(2)}, u32[]{:S(2)}) async-start(f32[16,1,864]{2,1,0:T(1,128)} %broadcast_in_dim.6), calls=%async_computation.1 | async-start | bytes 114688 | tf_op jit(solution)/shard_map/all_to_all | solution.py:27
  138.1 34.2 %all-to-all-start.2 = ((f32[64,1,864]{2,1,0:T(1,128)}), f32[64,1,864]{2,1,0:T(1,128)}, u32[]{:S(2)}, u32[]{:S(2)}) async-start(f32[64,1,864]{2,1,0:T(1,128)} %broadcast_in_dim.7), calls=%async_computation.2 | async-start | bytes 458752 | tf_op jit(solution)/shard_map/all_to_all | solution.py:27
  149.7 2.1 %copy-start = (bf16[1,32,2,16,128]{1,3,4,2,0:T(8,128)(2,1)S(1)}, bf16[1,32,2,16,128]{1,3,4,2,0:T(8,128)(2,1)}, u32[]{:S(2)}) copy-start(bf16[1,32,2,16,128]{1,3,4,2,0:T(8,128)(2,1)} %slice_bitcast_fusion) | copy-start | bytes 786436

commit v4 on v0

--- a/solution.py
+++ b/solution.py
@@ -18,8 +18,8 @@
 
 def summed_on_arrival(x, axis, dim):
     parts = in_blocks(x, dim, lax.axis_size(axis))
-    arrived = lax.all_to_all(parts, axis, split_axis=0, concat_axis=0, tiled=True)
-    return arrived.sum(axis=0)
+    arrived = lax.all_to_all(parts.astype(jnp.bfloat16), axis, split_axis=0, concat_axis=0, tiled=True)
+    return arrived.astype(jnp.float32).sum(axis=0)
 
 
 def sent_to_all(x, axis):
@@ -28,8 +28,8 @@
 
 
 def taken_together(x, axis):
-    everything = sent_to_all(x, axis)
-    return jnp.sum(everything, axis=0)
+    everything = sent_to_all(x.astype(jnp.bfloat16), axis)
+    return jnp.sum(everything.astype(jnp.float32), axis=0)
 
 
 def laid_out(parts, dim):
@@ -39,8 +39,8 @@
 
 
 def gathered_copies(x, axis, dim):
-    parts = sent_to_all(x, axis)
-    return laid_out(parts, dim)
+    parts = sent_to_all(x.astype(jnp.bfloat16), axis)
+    return laid_out(parts.astype(jnp.float32), dim)
 
 
 def convolve(inputs, weights, low, high):

time: 129 us -> 124 us (0.961)
  waiting for transfers between devices: 45.8 us -> 39 us
  other arithmetic: 0.3 us -> 3.32 us
  local copies, waits for them, and re-layouts: 22.6 us -> 21.1 us
    all_to_all x1, waiting for transfers between devices: 24.9 us -> 16.4 us  [summed_on_arrival(): lax.all_to_all(parts.astype(jnp.bfloat16), axis, split_axis=0, concat_axi...]
    unnamed x14 -> x21, local copies, waits for them, and re-layouts: 7.32 us -> 9.93 us
    slice x4, local copies, waits for them, and re-layouts: 4.21 us -> 1.96 us  [per_device(): grad_input = grad_extended[:, :, 1:]]
    broadcast_in_dim x0 -> x2, other arithmetic: none -> 2.17 us  [sent_to_all(): copies = jnp.broadcast_to(x, (lax.axis_size(axis), *x.shape))]
    all_to_all x2, waiting for transfers between devices: 19.7 us -> 21.3 us  [sent_to_all(): return lax.all_to_all(copies, axis, split_axis=0, concat_axis=0, tiled=True)]
    broadcast_in_dim x2, local copies, waits for them, and re-layouts: 1.46 us -> 0.16 us  [sent_to_all(): copies = jnp.broadcast_to(x, (lax.axis_size(axis), *x.shape))]
  transfers between devices with their start and end apart: 5 -> 5, of which waited for: 4 -> 4; matrix products, arithmetic and copies ran while one was open for 11% -> 17% of each run, Pallas kernels for 0% -> 0%
where the time goes in v4:
time: 124 us
  starting transfers between devices  49.4 us (40%)
  waiting for transfers between devices  39 us (31%)
  local copies, waits for them, and re-layouts  21.1 us (17%)
  matrix products  9.87 us (8%)
  other arithmetic  3.32 us (3%)
    all_to_all x1, starting transfers between devices, summed_on_arrival(): lax.all_to_all(parts.astype(jnp.bfloat16), axis, split_axis=0, concat_axi...  24.5 us
    all_to_all x2, waiting for transfers between devices, sent_to_all(): return lax.all_to_all(copies, axis, split_axis=0, concat_axis=0, tiled=True)  21.3 us
    all_to_all x1, waiting for transfers between devices, summed_on_arrival(): lax.all_to_all(parts.astype(jnp.bfloat16), axis, split_axis=0, concat_axi...  16.4 us
    ppermute x2, starting transfers between devices, from_behind(): return lax.ppermute(block, axis, route)  13.1 us
    all_to_all x2, starting transfers between devices, sent_to_all(): return lax.all_to_all(copies, axis, split_axis=0, concat_axis=0, tiled=True)  11.8 us
    unnamed x21, local copies, waits for them, and re-layouts  9.93 us
    conv_general_dilated x1, matrix products, weight_grad(): lax.conv_general_dilated(inputs, grads, (1, 1, 1), [(0, 0), (1, 0), (1, 0...  6.52 us
    concatenate x3, local copies, waits for them, and re-layouts, per_device(): extended = jnp.concatenate([below, volume], axis=2)  4.93 us
  transfers between devices with their start and end apart: 5, of which 4 were waited for; matrix products, arithmetic and copies ran while one was open for 17% of the time, Pallas kernels for 0%

profile of v4, /device:TPU:65, one launch (start us, length us, event | category | flops | bytes accessed | tf_op | source)
XLA Modules:
  0.0 123.6 jit_solution(14395078088103098685)
XLA Ops:
  0.6 0.0 copy-start
  0.6 1.0 slice.40
  1.6 11.2 %collective-permute-start = (bf16[1,32,1,16,128]{4,3,2,1,0:T(8,128)(2,1)S(1)}, bf16[1,32,1,16,128]{4,3,2,1,0:T(8,128)(2,1)S(1)}, u32[]{:S(2)}, u32[]{:S(2)}) collective-permute-start(bf16[1,32,1,16,128]{4,3,2,1,0:T(8,128)(2,1)S(1)} %slice.40), channel_id=1, source_target_pairs={{0,1},{1,2},{2,3},{3,4},{4,5},{5,6},{6,7},{7,8},{8,9},{9,10},{10,1... | collective-permute-start | bytes 393224 | tf_op jit(solution)/shard_map/ppermute | solution.py:10
  12.8 1.1 copy.98
  13.9 1.3 %collective-permute-done = bf16[1,32,1,16,128]{4,3,2,1,0:T(8,128)(2,1)S(1)} collective-permute-done((bf16[1,32,1,16,128]{4,3,2,1,0:T(8,128)(2,1)S(1)}, bf16[1,32,1,16,128]{4,3,2,1,0:T(8,128)(2,1)S(1)}, u32[]{:S(2)}, u32[]{:S(2)}) %collective-permute-start) | collective-permute-done | bytes 131104 | tf_op jit(solution)/shard_map/ppermute | solution.py:10
  15.2 1.0 constant_dynamic-update-slice_fusion
  16.2 3.6 %copy.107 = bf16[1,32,3,16,128]{1,0,4,3,2:T(2,128)(2,1)} copy(bf16[1,32,3,16,128]{4,3,2,1,0:T(8,128)(2,1)S(1)} %constant_dynamic-update-slice_fusion) | data formatting | bytes 786432 | tf_op jit(solution)/shard_map/concatenate | solution.py:84
  19.8 1.2 copy.118
  21.0 0.3 pad.2.clone
  21.3 0.7 copy.96
  22.0 0.1 slice.51
  22.1 1.3 %multiply_add_fusion = (f32[1,8,8,9,64]{4,2,3,1,0:T(8,128)S(1)}, bf16[1,8,8,9,64]{4,2,3,1,0:T(8,128)(2,1)S(1)}) fusion(bf16[64,32,3,3,3]{0,1,4,3,2:T(8,128)(2,1)S(1)} %copy-done, bf16[32,3,16,1,7,2]{0,4,5,2,1,3:T(8,128)(2,1)S(1)} %slice.51, bf16[32,3,16,1,8,18]{0,4,5,2,1,3:T(8,128)(2,1)S(1)} %copy.96, pred[8,9]{0,1:T(8,128)(4,1)S(1)} %copy-done.3), kind=kOutput, calls=%fused_computation.21 | convolution fusion | flops 63111168 | bytes 817224 | tf_op jit(solution)/shard_map/conv_general_dilated | solution.py:47
  23.5 0.1 copy.99
  23.6 1.9 %collective-permute-start.1 = (bf16[1,64,1,8,64]{1,3,4,0,2:T(8,128)(2,1)S(1)}, bf16[1,64,1,8,64]{1,3,4,0,2:T(8,128)(2,1)S(1)}, u32[]{:S(2)}, u32[]{:S(2)}) collective-permute-start(bf16[1,64,1,8,64]{1,3,4,0,2:T(8,128)(2,1)S(1)} %fusion.17), channel_id=1, source_target_pairs={{1,0},{2,1},{3,2},{4,3},{5,4},{6,5},{7,6},{8,7},{9,8},{10,9},{11,1... | collective-permute-start | bytes 196616 | tf_op jit(solution)/shard_map/ppermute | solution.py:10
  25.6 6.5 %convolution_convert_fusion = bf16[64,32,3,3,3]{0,1,4,3,2:T(8,128)(2,1)S(1)} fusion(bf16[1,32,3,16,128]{1,0,4,3,2:T(2,128)(2,1)S(1)} %copy-done.1, bf16[1,64,1,8,64]{1,3,4,0,2:T(8,128)(2,1)S(1)} %fusion.17), kind=kOutput, calls=%fused_computation.9 | convolution fusion | flops 54036480 | bytes 569344 | tf_op jit(solution)/shard_map/conv_general_dilated | solution.py:71
  32.2 0.2 copy.109
  32.3 0.2 convert_element_type.39
  32.5 0.5 broadcast.98
  33.0 0.8 reduce.6
  33.8 0.1 copy.122
  33.9 0.8 reshape.108
  34.8 24.5 %all-to-all-start = ((bf16[64,2,432]{2,1,0:T(2,128)(2,1)}), bf16[64,2,432]{2,1,0:T(2,128)(2,1)S(1)}, u32[]{:S(2)}, u32[]{:S(2)}) async-start(bf16[64,2,432]{2,1,0:T(2,128)(2,1)} %reshape.108), calls=%async_computation | async-start | bytes 262144 | tf_op jit(solution)/shard_map/all_to_all | solution.py:21
  59.3 1.2 convolution_select_fusion
  60.5 0.8 copy.102
  61.2 1.2 slice_bitcast_fusion
  62.4 16.4 %all-to-all-done = bf16[64,2,432]{2,1,0:T(2,128)(2,1)S(1)} async-done(((bf16[64,2,432]{2,1,0:T(2,128)(2,1)}), bf16[64,2,432]{2,1,0:T(2,128)(2,1)S(1)}, u32[]{:S(2)}, u32[]{:S(2)}) %all-to-all-start) | async-done | bytes 110624 | tf_op jit(solution)/shard_map/all_to_all | solution.py:21
  78.8 0.2 reshape.109
  79.0 0.2 reduce_sum.24
  79.3 0.8 reduce.7
  80.1 0.7 reshape.110
  80.8 5.9 %all-to-all-start.1 = ((bf16[16,2,432]{2,1,0:T(2,128)(2,1)}), bf16[16,2,432]{2,1,0:T(2,128)(2,1)S(1)}, u32[]{:S(2)}, u32[]{:S(2)}) async-start(bf16[16,2,432]{2,1,0:T(2,128)(2,1)} %reshape.110), calls=%async_computation.1 | async-start | bytes 65536 | tf_op jit(solution)/shard_map/all_to_all | solution.py:27
  86.7 0.8 copy.114
  87.6 4.8 %all-to-all-done.1 = bf16[16,2,432]{2,1,0:T(2,128)(2,1)S(1)} async-done(((bf16[16,2,432]{2,1,0:T(2,128)(2,1)}), bf16[16,2,432]{2,1,0:T(2,128)(2,1)S(1)}, u32[]{:S(2)}, u32[]{:S(2)}) %all-to-all-start.1) | async-done | bytes 27680 | tf_op jit(solution)/shard_map/all_to_all | solution.py:27
  92.4 0.1 reshape.111
  92.5 0.1 reduce_sum.25
  92.6 0.1 broadcast_in_dim.7
  92.7 1.4 %reduce.8 = bf16[64,864]{1,0:T(8,128)(2,1)S(1)} reduce(bf16[64,1,864]{2,1,0:T(2,128)(2,1)S(1)} %broadcast_in_dim.7, bf16[]{:T(256)} %broadcast.98), dimensions={1}, to_apply=%broadcast_in_dim.7.reduce_sub_computation | reduce | bytes 221186 | tf_op jit(solution)/shard_map/broadcast_in_dim | solution.py:26
  94.1 0.8 reshape.112
  94.9 5.9 %all-to-all-start.2 = ((bf16[64,2,432]{2,1,0:T(2,128)(2,1)}), bf16[64,2,432]{2,1,0:T(2,128)(2,1)S(1)}, u32[]{:S(2)}, u32[]{:S(2)}) async-start(bf16[64,2,432]{2,1,0:T(2,128)(2,1)} %reshape.112), calls=%async_computation.2 | async-start | bytes 262144 | tf_op jit(solution)/shard_map/all_to_all | solution.py:27
  100.8 0.8 fusion.5
  101.6 0.2 copy.105
  101.8 0.8 fusion.9
  102.6 2.9 %copy.115 = bf16[1,32,2,16,128]{4,3,2,1,0:T(8,128)(2,1)} copy(bf16[1,32,2,16,128]{1,3,4,2,0:T(8,128)(2,1)} %fusion.9) | data formatting | bytes 524288
  105.6 16.5 %all-to-all-done.2 = bf16[64,2,432]{2,1,0:T(2,128)(2,1)S(1)} async-done(((bf16[64,2,432]{2,1,0:T(2,128)(2,1)}), bf16[64,2,432]{2,1,0:T(2,128)(2,1)S(1)}, u32[]{:S(2)}, u32[]{:S(2)}) %all-to-all-start.2) | async-done | bytes 110624 | tf_op jit(solution)/shard_map/all_to_all | solution.py:27
  122.1 0.2 reshape.113
  122.4 0.2 copy.113
  122.6 0.2 div.14
  122.8 0.8 copy.116
  (20 shorter events, 0.3 us)
Async XLA Ops:
  0.6 21.5 %copy-start = (bf16[64,32,3,3,3]{0,1,4,3,2:T(8,128)(2,1)S(1)}, bf16[64,32,3,3,3]{0,1,4,3,2:T(8,128)(2,1)}, u32[]{:S(2)}) copy-start(bf16[64,32,3,3,3]{0,1,4,3,2:T(8,128)(2,1)} %param.6) | copy-start | bytes 331780
  1.6 13.6 %collective-permute-start = (bf16[1,32,1,16,128]{4,3,2,1,0:T(8,128)(2,1)S(1)}, bf16[1,32,1,16,128]{4,3,2,1,0:T(8,128)(2,1)S(1)}, u32[]{:S(2)}, u32[]{:S(2)}) collective-permute-start(bf16[1,32,1,16,128]{4,3,2,1,0:T(8,128)(2,1)S(1)} %slice.40), channel_id=1, source_target_pairs={{0,1},{1,2},{2,3},{3,4},{4,5},{5,6},{6,7},{7,8},{8,9},{9,10},{10,1... | collective-permute-start | bytes 393224 | tf_op jit(solution)/shard_map/ppermute | solution.py:10
  21.3 0.8 copy-start.3
  22.1 3.5 %copy-start.1 = (bf16[1,32,3,16,128]{1,0,4,3,2:T(2,128)(2,1)S(1)}, bf16[1,32,3,16,128]{1,0,4,3,2:T(2,128)(2,1)}, u32[]{:S(2)}) copy-start(bf16[1,32,3,16,128]{1,0,4,3,2:T(2,128)(2,1)} %copy.107) | copy-start | bytes 1179652
  23.6 64.0 %collective-permute-start.1 = (bf16[1,64,1,8,64]{1,3,4,0,2:T(8,128)(2,1)S(1)}, bf16[1,64,1,8,64]{1,3,4,0,2:T(8,128)(2,1)S(1)}, u32[]{:S(2)}, u32[]{:S(2)}) collective-permute-start(bf16[1,64,1,8,64]{1,3,4,0,2:T(8,128)(2,1)S(1)} %fusion.17), channel_id=1, source_target_pairs={{1,0},{2,1},{3,2},{4,3},{5,4},{6,5},{7,6},{8,7},{9,8},{10,9},{11,1... | collective-permute-start | bytes 196616 | tf_op jit(solution)/shard_map/ppermute | solution.py:10
  32.1 27.1 %copy-start.2 = (pred[8,18]{0,1:T(8,128)(4,1)S(1)}, pred[8,18]{0,1:T(8,128)(4,1)}, u32[]{:S(2)}) copy-start(pred[8,18]{0,1:T(8,128)(4,1)} %constant.60) | copy-start | bytes 436
  34.8 44.0 %all-to-all-start = ((bf16[64,2,432]{2,1,0:T(2,128)(2,1)}), bf16[64,2,432]{2,1,0:T(2,128)(2,1)S(1)}, u32[]{:S(2)}, u32[]{:S(2)}) async-start(bf16[64,2,432]{2,1,0:T(2,128)(2,1)} %reshape.108), calls=%async_computation | async-start | bytes 262144 | tf_op jit(solution)/shard_map/all_to_all | solution.py:21
  80.8 11.6 %all-to-all-start.1 = ((bf16[16,2,432]{2,1,0:T(2,128)(2,1)}), bf16[16,2,432]{2,1,0:T(2,128)(2,1)S(1)}, u32[]{:S(2)}, u32[]{:S(2)}) async-start(bf16[16,2,432]{2,1,0:T(2,128)(2,1)} %reshape.110), calls=%async_computation.1 | async-start | bytes 65536 | tf_op jit(solution)/shard_map/all_to_all | solution.py:27
  94.9 27.2 %all-to-all-start.2 = ((bf16[64,2,432]{2,1,0:T(2,128)(2,1)}), bf16[64,2,432]{2,1,0:T(2,128)(2,1)S(1)}, u32[]{:S(2)}, u32[]{:S(2)}) async-start(bf16[64,2,432]{2,1,0:T(2,128)(2,1)} %reshape.112), calls=%async_computation.2 | async-start | bytes 262144 | tf_op jit(solution)/shard_map/all_to_all | solution.py:27

commit v5 on v4

--- a/solution.py
+++ b/solution.py
@@ -90,11 +90,12 @@
     grad_extended = input_grad(local_grad, kernel, 2, 2)
     kernel_local = weight_grad(extended, local_grad)
     grad_input = grad_extended[:, :, 1:]
-    next_grad = from_behind(local_grad[:, :, :1], "space", -1)
+    flat_terms = kernel_local.reshape(-1)
+    share = summed_on_arrival(flat_terms, "space", 0)
+    first_grad, share = lax.optimization_barrier((local_grad[:, :, :1], share))
+    next_grad = from_behind(first_grad, "space", -1)
     from_above = input_grad(next_grad, kernel, 2, 0)
     grad_input = grad_input.at[:, :, -1:].add(from_above)
-    flat_terms = kernel_local.reshape(-1)
-    share = summed_on_arrival(flat_terms, "space", 0)
     share = taken_together(share, "dp")
     kernel_total = gathered_copies(share, "space", 0).reshape(kernel_local.shape)
     total_cells = (

time: 124 us -> 128 us (1.032)
  starting transfers between devices: 49.4 us -> 52.7 us
    all_to_all x2, starting transfers between devices: 11.8 us -> 15 us  [sent_to_all(): return lax.all_to_all(copies, axis, split_axis=0, concat_axis=0, tiled=True)]
    ppermute x2, waiting for transfers between devices: 1.31 us -> 3.4 us  [from_behind(): return lax.ppermute(block, axis, route)]
    all_to_all x2, waiting for transfers between devices: 21.3 us -> 19.3 us  [sent_to_all(): return lax.all_to_all(copies, axis, split_axis=0, concat_axis=0, tiled=True)]
  transfers between devices with their start and end apart: 5 -> 5, of which waited for: 4 -> 5; matrix products, arithmetic and copies ran while one was open for 17% -> 9% of each run, Pallas kernels for 0% -> 0%
where the time goes in v5:
time: 128 us; the launch traced here: 127 us
  starting transfers between devices  52.7 us (41%)
  waiting for transfers between devices  38.9 us (30%)
  local copies, waits for them, and re-layouts  21.5 us (17%)
  matrix products  9.86 us (8%)
  other arithmetic  3.33 us (3%)
    all_to_all x1, starting transfers between devices, summed_on_arrival(): lax.all_to_all(parts.astype(jnp.bfloat16), axis, split_axis=0, concat_axi...  24.4 us
    all_to_all x2, waiting for transfers between devices, sent_to_all(): return lax.all_to_all(copies, axis, split_axis=0, concat_axis=0, tiled=True)  19.3 us
    all_to_all x1, waiting for transfers between devices, summed_on_arrival(): lax.all_to_all(parts.astype(jnp.bfloat16), axis, split_axis=0, concat_axi...  16.3 us
    all_to_all x2, starting transfers between devices, sent_to_all(): return lax.all_to_all(copies, axis, split_axis=0, concat_axis=0, tiled=True)  15 us
    ppermute x2, starting transfers between devices, from_behind(): return lax.ppermute(block, axis, route)  13.3 us
    unnamed x21, local copies, waits for them, and re-layouts  10.4 us
    conv_general_dilated x1, matrix products, weight_grad(): lax.conv_general_dilated(inputs, grads, (1, 1, 1), [(0, 0), (1, 0), (1, 0...  6.52 us
    concatenate x3, local copies, waits for them, and re-layouts, per_device(): extended = jnp.concatenate([below, volume], axis=2)  4.93 us
  transfers between devices with their start and end apart: 5, of which 5 were waited for; matrix products, arithmetic and copies ran while one was open for 9% of the time, Pallas kernels for 0%

profile of v5, /device:TPU:65, one launch (start us, length us, event | category | flops | bytes accessed | tf_op | source)
XLA Modules:
  0.0 127.3 jit_solution(13490742194433065754)
XLA Ops:
  0.6 1.0 slice.40
  1.6 11.2 %collective-permute-start = (bf16[1,32,1,16,128]{4,3,2,1,0:T(8,128)(2,1)S(1)}, bf16[1,32,1,16,128]{4,3,2,1,0:T(8,128)(2,1)S(1)}, u32[]{:S(2)}, u32[]{:S(2)}) collective-permute-start(bf16[1,32,1,16,128]{4,3,2,1,0:T(8,128)(2,1)S(1)} %slice.40), channel_id=1, source_target_pairs={{0,1},{1,2},{2,3},{3,4},{4,5},{5,6},{6,7},{7,8},{8,9},{9,10},{10,1... | collective-permute-start | bytes 393224 | tf_op jit(solution)/shard_map/ppermute | solution.py:10
  12.8 1.1 copy.98
  13.9 1.3 %collective-permute-done = bf16[1,32,1,16,128]{4,3,2,1,0:T(8,128)(2,1)S(1)} collective-permute-done((bf16[1,32,1,16,128]{4,3,2,1,0:T(8,128)(2,1)S(1)}, bf16[1,32,1,16,128]{4,3,2,1,0:T(8,128)(2,1)S(1)}, u32[]{:S(2)}, u32[]{:S(2)}) %collective-permute-start) | collective-permute-done | bytes 131104 | tf_op jit(solution)/shard_map/ppermute | solution.py:10
  15.2 1.0 constant_dynamic-update-slice_fusion
  16.2 3.6 %copy.103 = bf16[1,32,3,16,128]{1,0,4,3,2:T(2,128)(2,1)} copy(bf16[1,32,3,16,128]{4,3,2,1,0:T(8,128)(2,1)S(1)} %constant_dynamic-update-slice_fusion) | data formatting | bytes 786432 | tf_op jit(solution)/shard_map/concatenate | solution.py:84
  19.8 1.2 copy.118
  21.0 0.3 pad.2.clone
  21.3 0.7 copy.96
  22.1 1.3 %multiply_add_fusion = (f32[1,8,8,9,64]{4,2,3,1,0:T(8,128)S(1)}, bf16[1,8,8,9,64]{4,2,3,1,0:T(8,128)(2,1)S(1)}) fusion(bf16[64,32,3,3,3]{0,1,4,3,2:T(8,128)(2,1)S(1)} %copy-done, bf16[32,3,16,1,7,2]{0,4,5,2,1,3:T(8,128)(2,1)S(1)} %slice.51, bf16[32,3,16,1,8,18]{0,4,5,2,1,3:T(8,128)(2,1)S(1)} %copy.96, pred[8,9]{0,1:T(8,128)(4,1)S(1)} %copy-done.3), kind=kOutput, calls=%fused_computation.21 | convolution fusion | flops 63111168 | bytes 817224 | tf_op jit(solution)/shard_map/conv_general_dilated | solution.py:47
  23.5 0.1 copy.99
  23.6 0.4 copy-done.1
  24.0 6.5 %convolution_convert_fusion = bf16[64,32,3,3,3]{0,1,4,3,2:T(8,128)(2,1)S(1)} fusion(bf16[1,32,3,16,128]{1,0,4,3,2:T(2,128)(2,1)S(1)} %copy-done.1, bf16[1,64,1,8,64]{1,3,4,0,2:T(8,128)(2,1)S(1)} %fusion.17), kind=kOutput, calls=%fused_computation.9 | convolution fusion | flops 54036480 | bytes 569344 | tf_op jit(solution)/shard_map/conv_general_dilated | solution.py:71
  30.5 0.2 copy.105
  30.7 0.2 convert_element_type.43
  30.9 0.5 broadcast.98
  31.4 0.8 reduce.5
  32.2 0.1 copy.122
  32.3 0.8 reshape.109
  33.1 24.4 %all-to-all-start = ((bf16[64,2,432]{2,1,0:T(2,128)(2,1)}), bf16[64,2,432]{2,1,0:T(2,128)(2,1)S(1)}, u32[]{:S(2)}, u32[]{:S(2)}) async-start(bf16[64,2,432]{2,1,0:T(2,128)(2,1)} %reshape.109), calls=%async_computation | async-start | bytes 262144 | tf_op jit(solution)/shard_map/all_to_all | solution.py:21
  57.6 1.2 convolution_select_fusion
  58.8 0.8 copy.102
  59.6 1.2 slice_bitcast_fusion
  60.8 16.3 %all-to-all-done = bf16[64,2,432]{2,1,0:T(2,128)(2,1)S(1)} async-done(((bf16[64,2,432]{2,1,0:T(2,128)(2,1)}), bf16[64,2,432]{2,1,0:T(2,128)(2,1)S(1)}, u32[]{:S(2)}, u32[]{:S(2)}) %all-to-all-start) | async-done | bytes 110624 | tf_op jit(solution)/shard_map/all_to_all | solution.py:21
  77.1 0.2 reshape.110
  77.3 0.2 convert_reduce_fusion
  77.5 2.1 %collective-permute-start.1 = (bf16[1,64,1,8,64]{1,3,4,0,2:T(8,128)(2,1)S(1)}, bf16[1,64,1,8,64]{1,3,4,0,2:T(8,128)(2,1)S(1)}, u32[]{:S(2)}, u32[]{:S(2)}) collective-permute-start(bf16[1,64,1,8,64]{1,3,4,0,2:T(8,128)(2,1)S(1)} %fusion.17), channel_id=1, source_target_pairs={{1,0},{2,1},{3,2},{4,3},{5,4},{6,5},{7,6},{8,7},{9,8},{10,9},{11,1... | collective-permute-start | bytes 196616 | tf_op jit(solution)/shard_map/ppermute | solution.py:10
  79.7 0.8 reduce.6
  80.5 0.7 reshape.111
  81.3 6.0 %all-to-all-start.1 = ((bf16[16,2,432]{2,1,0:T(2,128)(2,1)}), bf16[16,2,432]{2,1,0:T(2,128)(2,1)S(1)}, u32[]{:S(2)}, u32[]{:S(2)}) async-start(bf16[16,2,432]{2,1,0:T(2,128)(2,1)} %reshape.111), calls=%async_computation.1 | async-start | bytes 65536 | tf_op jit(solution)/shard_map/all_to_all | solution.py:27
  87.3 0.8 copy.114
  88.1 2.1 %collective-permute-done.1 = bf16[1,64,1,8,64]{1,3,4,0,2:T(8,128)(2,1)S(1)} collective-permute-done((bf16[1,64,1,8,64]{1,3,4,0,2:T(8,128)(2,1)S(1)}, bf16[1,64,1,8,64]{1,3,4,0,2:T(8,128)(2,1)S(1)}, u32[]{:S(2)}, u32[]{:S(2)}) %collective-permute-start.1) | collective-permute-done | bytes 65568 | tf_op jit(solution)/shard_map/ppermute | solution.py:10
  90.3 2.9 %all-to-all-done.1 = bf16[16,2,432]{2,1,0:T(2,128)(2,1)S(1)} async-done(((bf16[16,2,432]{2,1,0:T(2,128)(2,1)}), bf16[16,2,432]{2,1,0:T(2,128)(2,1)S(1)}, u32[]{:S(2)}, u32[]{:S(2)}) %all-to-all-start.1) | async-done | bytes 27680 | tf_op jit(solution)/shard_map/all_to_all | solution.py:27
  93.2 0.1 reshape.112
  93.3 0.1 reduce_sum.22
  93.4 0.1 broadcast_in_dim.7
  93.5 1.4 %reduce.7 = bf16[64,864]{1,0:T(8,128)(2,1)S(1)} reduce(bf16[64,1,864]{2,1,0:T(2,128)(2,1)S(1)} %broadcast_in_dim.7, bf16[]{:T(256)} %broadcast.98), dimensions={1}, to_apply=%broadcast_in_dim.7.reduce_sub_computation | reduce | bytes 221186 | tf_op jit(solution)/shard_map/broadcast_in_dim | solution.py:26
  94.9 0.8 reshape.113
  95.7 8.9 %all-to-all-start.2 = ((bf16[64,2,432]{2,1,0:T(2,128)(2,1)}), bf16[64,2,432]{2,1,0:T(2,128)(2,1)S(1)}, u32[]{:S(2)}, u32[]{:S(2)}) async-start(bf16[64,2,432]{2,1,0:T(2,128)(2,1)} %reshape.113), calls=%async_computation.2 | async-start | bytes 262144 | tf_op jit(solution)/shard_map/all_to_all | solution.py:27
  104.6 0.8 fusion.5
  105.5 0.2 copy.109
  105.6 0.8 fusion.9
  106.5 2.9 %copy.115 = bf16[1,32,2,16,128]{4,3,2,1,0:T(8,128)(2,1)} copy(bf16[1,32,2,16,128]{1,3,4,2,0:T(8,128)(2,1)} %fusion.9) | data formatting | bytes 524288
  109.4 16.4 %all-to-all-done.2 = bf16[64,2,432]{2,1,0:T(2,128)(2,1)S(1)} async-done(((bf16[64,2,432]{2,1,0:T(2,128)(2,1)}), bf16[64,2,432]{2,1,0:T(2,128)(2,1)S(1)}, u32[]{:S(2)}, u32[]{:S(2)}) %all-to-all-start.2) | async-done | bytes 110624 | tf_op jit(solution)/shard_map/all_to_all | solution.py:27
  125.8 0.2 reshape.114
  126.1 0.2 copy.113
  126.3 0.2 div.14
  126.5 0.8 copy.116
  (20 shorter events, 0.3 us)
Async XLA Ops:
  0.6 21.5 %copy-start = (bf16[64,32,3,3,3]{0,1,4,3,2:T(8,128)(2,1)S(1)}, bf16[64,32,3,3,3]{0,1,4,3,2:T(8,128)(2,1)}, u32[]{:S(2)}) copy-start(bf16[64,32,3,3,3]{0,1,4,3,2:T(8,128)(2,1)} %param.6) | copy-start | bytes 331780
  1.6 13.6 %collective-permute-start = (bf16[1,32,1,16,128]{4,3,2,1,0:T(8,128)(2,1)S(1)}, bf16[1,32,1,16,128]{4,3,2,1,0:T(8,128)(2,1)S(1)}, u32[]{:S(2)}, u32[]{:S(2)}) collective-permute-start(bf16[1,32,1,16,128]{4,3,2,1,0:T(8,128)(2,1)S(1)} %slice.40), channel_id=1, source_target_pairs={{0,1},{1,2},{2,3},{3,4},{4,5},{5,6},{6,7},{7,8},{8,9},{9,10},{10,1... | collective-permute-start | bytes 393224 | tf_op jit(solution)/shard_map/ppermute | solution.py:10
  21.3 0.8 copy-start.3
  22.1 1.9 %copy-start.1 = (bf16[1,32,3,16,128]{1,0,4,3,2:T(2,128)(2,1)S(1)}, bf16[1,32,3,16,128]{1,0,4,3,2:T(2,128)(2,1)}, u32[]{:S(2)}) copy-start(bf16[1,32,3,16,128]{1,0,4,3,2:T(2,128)(2,1)} %copy.103) | copy-start | bytes 1179652
  30.5 27.1 %copy-start.2 = (pred[8,18]{0,1:T(8,128)(4,1)S(1)}, pred[8,18]{0,1:T(8,128)(4,1)}, u32[]{:S(2)}) copy-start(pred[8,18]{0,1:T(8,128)(4,1)} %constant.59) | copy-start | bytes 436
  33.1 43.9 %all-to-all-start = ((bf16[64,2,432]{2,1,0:T(2,128)(2,1)}), bf16[64,2,432]{2,1,0:T(2,128)(2,1)S(1)}, u32[]{:S(2)}, u32[]{:S(2)}) async-start(bf16[64,2,432]{2,1,0:T(2,128)(2,1)} %reshape.109), calls=%async_computation | async-start | bytes 262144 | tf_op jit(solution)/shard_map/all_to_all | solution.py:21
  77.5 12.7 %collective-permute-start.1 = (bf16[1,64,1,8,64]{1,3,4,0,2:T(8,128)(2,1)S(1)}, bf16[1,64,1,8,64]{1,3,4,0,2:T(8,128)(2,1)S(1)}, u32[]{:S(2)}, u32[]{:S(2)}) collective-permute-start(bf16[1,64,1,8,64]{1,3,4,0,2:T(8,128)(2,1)S(1)} %fusion.17), channel_id=1, source_target_pairs={{1,0},{2,1},{3,2},{4,3},{5,4},{6,5},{7,6},{8,7},{9,8},{10,9},{11,1... | collective-permute-start | bytes 196616 | tf_op jit(solution)/shard_map/ppermute | solution.py:10
  81.3 11.9 %all-to-all-start.1 = ((bf16[16,2,432]{2,1,0:T(2,128)(2,1)}), bf16[16,2,432]{2,1,0:T(2,128)(2,1)S(1)}, u32[]{:S(2)}, u32[]{:S(2)}) async-start(bf16[16,2,432]{2,1,0:T(2,128)(2,1)} %reshape.111), calls=%async_computation.1 | async-start | bytes 65536 | tf_op jit(solution)/shard_map/all_to_all | solution.py:27
  95.7 30.1 %all-to-all-start.2 = ((bf16[64,2,432]{2,1,0:T(2,128)(2,1)}), bf16[64,2,432]{2,1,0:T(2,128)(2,1)S(1)}, u32[]{:S(2)}, u32[]{:S(2)}) async-start(bf16[64,2,432]{2,1,0:T(2,128)(2,1)} %reshape.113), calls=%async_computation.2 | async-start | bytes 262144 | tf_op jit(solution)/shard_map/all_to_all | solution.py:27

commit v6 on v0

--- a/solution.py
+++ b/solution.py
@@ -39,8 +39,8 @@
 
 
 def gathered_copies(x, axis, dim):
-    parts = sent_to_all(x, axis)
-    return laid_out(parts, dim)
+    parts = sent_to_all(x.astype(jnp.bfloat16), axis)
+    return laid_out(parts.astype(jnp.float32), dim)
 
 
 def convolve(inputs, weights, low, high):

time: 129 us -> 127 us (0.984)
  local copies, waits for them, and re-layouts: 22.6 us -> 21.1 us
  waiting for transfers between devices: 45.8 us -> 44.3 us
  other arithmetic: 0.3 us -> 1.67 us
    all_to_all x1, waiting for transfers between devices: 24.9 us -> 21.5 us  [summed_on_arrival(): lax.all_to_all(parts, axis, split_axis=0, concat_axis=0, tiled=True)]
    slice x4, local copies, waits for them, and re-layouts: 4.21 us -> 1.94 us  [per_device(): grad_input = grad_extended[:, :, 1:]]
    all_to_all x2, waiting for transfers between devices: 19.7 us -> 21.4 us  [sent_to_all(): return lax.all_to_all(copies, axis, split_axis=0, concat_axis=0, tiled=True)]
    broadcast_in_dim x0 -> x1, other arithmetic: none -> 1.36 us  [sent_to_all(): copies = jnp.broadcast_to(x, (lax.axis_size(axis), *x.shape))]
    unnamed x14 -> x16, local copies, waits for them, and re-layouts: 7.32 us -> 8.33 us
  transfers between devices with their start and end apart: 5 -> 5, of which waited for: 4 -> 4; matrix products, arithmetic and copies ran while one was open for 11% -> 8% of each run, Pallas kernels for 0% -> 0%
where the time goes in v6:
time: 127 us
  starting transfers between devices  49.1 us (39%)
  waiting for transfers between devices  44.3 us (35%)
  local copies, waits for them, and re-layouts  21.1 us (17%)
  matrix products  9.83 us (8%)
  other arithmetic  1.67 us (1%)
    all_to_all x1, starting transfers between devices, summed_on_arrival(): lax.all_to_all(parts, axis, split_axis=0, concat_axis=0, tiled=True)  24.4 us
    all_to_all x1, waiting for transfers between devices, summed_on_arrival(): lax.all_to_all(parts, axis, split_axis=0, concat_axis=0, tiled=True)  21.5 us
    all_to_all x2, waiting for transfers between devices, sent_to_all(): return lax.all_to_all(copies, axis, split_axis=0, concat_axis=0, tiled=True)  21.4 us
    ppermute x2, starting transfers between devices, from_behind(): return lax.ppermute(block, axis, route)  13.7 us
    all_to_all x2, starting transfers between devices, sent_to_all(): return lax.all_to_all(copies, axis, split_axis=0, concat_axis=0, tiled=True)  11 us
    unnamed x16, local copies, waits for them, and re-layouts  8.33 us
    conv_general_dilated x1, matrix products, weight_grad(): lax.conv_general_dilated(inputs, grads, (1, 1, 1), [(0, 0), (1, 0), (1, 0...  6.49 us
    concatenate x3, local copies, waits for them, and re-layouts, per_device(): extended = jnp.concatenate([below, volume], axis=2)  4.91 us
  transfers between devices with their start and end apart: 5, of which 4 were waited for; matrix products, arithmetic and copies ran while one was open for 8% of the time, Pallas kernels for 0%

profile of v6, /device:TPU:65, one launch (start us, length us, event | category | flops | bytes accessed | tf_op | source)
XLA Modules:
  0.0 126.9 jit_solution(10780232782149587917)
XLA Ops:
  0.6 0.0 copy-start
  0.6 1.0 slice.40
  1.6 11.2 %collective-permute-start = (bf16[1,32,1,16,128]{4,3,2,1,0:T(8,128)(2,1)S(1)}, bf16[1,32,1,16,128]{4,3,2,1,0:T(8,128)(2,1)S(1)}, u32[]{:S(2)}, u32[]{:S(2)}) collective-permute-start(bf16[1,32,1,16,128]{4,3,2,1,0:T(8,128)(2,1)S(1)} %slice.40), channel_id=1, source_target_pairs={{0,1},{1,2},{2,3},{3,4},{4,5},{5,6},{6,7},{7,8},{8,9},{9,10},{10,1... | collective-permute-start | bytes 393224 | tf_op jit(solution)/shard_map/ppermute | solution.py:10
  12.8 1.1 copy.98
  13.9 1.3 %collective-permute-done = bf16[1,32,1,16,128]{4,3,2,1,0:T(8,128)(2,1)S(1)} collective-permute-done((bf16[1,32,1,16,128]{4,3,2,1,0:T(8,128)(2,1)S(1)}, bf16[1,32,1,16,128]{4,3,2,1,0:T(8,128)(2,1)S(1)}, u32[]{:S(2)}, u32[]{:S(2)}) %collective-permute-start) | collective-permute-done | bytes 131104 | tf_op jit(solution)/shard_map/ppermute | solution.py:10
  15.2 1.0 constant_dynamic-update-slice_fusion
  16.2 3.6 %copy.107 = bf16[1,32,3,16,128]{1,0,4,3,2:T(2,128)(2,1)} copy(bf16[1,32,3,16,128]{4,3,2,1,0:T(8,128)(2,1)S(1)} %constant_dynamic-update-slice_fusion) | data formatting | bytes 786432 | tf_op jit(solution)/shard_map/concatenate | solution.py:84
  19.8 1.2 copy.118
  21.0 0.3 pad.2.clone
  21.3 0.0 copy-start.3
  21.3 0.7 copy.96
  22.0 0.1 slice.51
  22.1 0.0 copy-done
  22.1 1.3 %multiply_add_fusion = (f32[1,8,8,9,64]{4,2,3,1,0:T(8,128)S(1)}, bf16[1,8,8,9,64]{4,2,3,1,0:T(8,128)(2,1)S(1)}) fusion(bf16[64,32,3,3,3]{0,1,4,3,2:T(8,128)(2,1)S(1)} %copy-done, bf16[32,3,16,1,7,2]{0,4,5,2,1,3:T(8,128)(2,1)S(1)} %slice.51, bf16[32,3,16,1,8,18]{0,4,5,2,1,3:T(8,128)(2,1)S(1)} %copy.96, pred[8,9]{0,1:T(8,128)(4,1)S(1)} %copy-done.3), kind=kOutput, calls=%fused_computation.20 | convolution fusion | flops 63111168 | bytes 817224 | tf_op jit(solution)/shard_map/conv_general_dilated | solution.py:47
  23.4 0.1 copy.99
  23.5 0.4 copy-done.1
  24.0 6.5 %fusion.18 = f32[64,32,3,3,3]{0,1,4,3,2:T(8,128)S(1)} fusion(bf16[1,32,3,16,128]{1,0,4,3,2:T(2,128)(2,1)S(1)} %copy-done.1, bf16[1,64,1,8,64]{1,3,4,0,2:T(8,128)(2,1)S(1)} %fusion.17), kind=kOutput, calls=%fused_computation.24 | convolution fusion | flops 53981184 | bytes 679936 | tf_op jit(solution)/shard_map/conv_general_dilated | solution.py:71
  30.5 0.0 copy-start.2
  30.5 0.3 copy.109
  30.8 0.2 all_to_all.14
  31.0 0.9 copy.110
  31.9 24.4 %all-to-all-start = ((f32[64,1,864]{2,1,0:T(1,128)}), f32[64,1,864]{2,1,0:T(1,128)S(1)}, u32[]{:S(2)}, u32[]{:S(2)}) async-start(f32[64,1,864]{2,1,0:T(1,128)} %copy.110), calls=%async_computation | async-start | bytes 458752 | tf_op jit(solution)/shard_map/all_to_all | solution.py:21
  56.3 2.5 %collective-permute-start.1 = (bf16[1,64,1,8,64]{1,3,4,0,2:T(8,128)(2,1)S(1)}, bf16[1,64,1,8,64]{1,3,4,0,2:T(8,128)(2,1)S(1)}, u32[]{:S(2)}, u32[]{:S(2)}) collective-permute-start(bf16[1,64,1,8,64]{1,3,4,0,2:T(8,128)(2,1)S(1)} %fusion.17), channel_id=1, source_target_pairs={{1,0},{2,1},{3,2},{4,3},{5,4},{6,5},{7,6},{8,7},{9,8},{10,9},{11,1... | collective-permute-start | bytes 196616 | tf_op jit(solution)/shard_map/ppermute | solution.py:10
  59.0 1.2 convolution_select_fusion
  60.1 0.8 copy.102
  60.9 1.1 slice_bitcast_fusion
  62.1 21.5 %all-to-all-done = f32[64,1,864]{2,1,0:T(1,128)S(1)} async-done(((f32[64,1,864]{2,1,0:T(1,128)}), f32[64,1,864]{2,1,0:T(1,128)S(1)}, u32[]{:S(2)}, u32[]{:S(2)}) %all-to-all-start) | async-done | bytes 221216 | tf_op jit(solution)/shard_map/all_to_all | solution.py:21
  83.6 0.2 reduce_sum.18
  83.8 0.7 broadcast_in_dim.6
  84.4 5.2 %all-to-all-start.1 = ((f32[16,1,864]{2,1,0:T(1,128)}), f32[16,1,864]{2,1,0:T(1,128)S(1)}, u32[]{:S(2)}, u32[]{:S(2)}) async-start(f32[16,1,864]{2,1,0:T(1,128)} %broadcast_in_dim.6), calls=%async_computation.1 | async-start | bytes 114688 | tf_op jit(solution)/shard_map/all_to_all | solution.py:27
  89.7 0.8 copy.114
  90.5 0.0 collective-permute-done.1
  90.6 4.8 %all-to-all-done.1 = f32[16,1,864]{2,1,0:T(1,128)S(1)} async-done(((f32[16,1,864]{2,1,0:T(1,128)}), f32[16,1,864]{2,1,0:T(1,128)S(1)}, u32[]{:S(2)}, u32[]{:S(2)}) %all-to-all-start.1) | async-done | bytes 55328 | tf_op jit(solution)/shard_map/all_to_all | solution.py:27
  95.4 0.1 reduce_sum.19
  95.5 0.1 broadcast_in_dim.7
  95.6 0.5 broadcast.99
  96.1 1.4 %reduce.4 = bf16[64,864]{1,0:T(8,128)(2,1)S(1)} reduce(bf16[64,1,864]{2,1,0:T(2,128)(2,1)S(1)} %broadcast_in_dim.7, bf16[]{:T(256)} %broadcast.99), dimensions={1}, to_apply=%broadcast_in_dim.7.reduce_sub_computation | reduce | bytes 221186 | tf_op jit(solution)/shard_map/broadcast_in_dim | solution.py:26
  97.5 0.8 reshape.98
  98.3 5.8 %all-to-all-start.2 = ((bf16[64,2,432]{2,1,0:T(2,128)(2,1)}), bf16[64,2,432]{2,1,0:T(2,128)(2,1)S(1)}, u32[]{:S(2)}, u32[]{:S(2)}) async-start(bf16[64,2,432]{2,1,0:T(2,128)(2,1)} %reshape.98), calls=%async_computation.2 | async-start | bytes 262144 | tf_op jit(solution)/shard_map/all_to_all | solution.py:27
  104.1 0.8 fusion.5
  105.0 0.2 copy.105
  105.1 0.8 fusion.9
  105.9 2.9 %copy.115 = bf16[1,32,2,16,128]{4,3,2,1,0:T(8,128)(2,1)} copy(bf16[1,32,2,16,128]{1,3,4,2,0:T(8,128)(2,1)} %fusion.9) | data formatting | bytes 524288
  108.9 16.6 %all-to-all-done.2 = bf16[64,2,432]{2,1,0:T(2,128)(2,1)S(1)} async-done(((bf16[64,2,432]{2,1,0:T(2,128)(2,1)}), bf16[64,2,432]{2,1,0:T(2,128)(2,1)S(1)}, u32[]{:S(2)}, u32[]{:S(2)}) %all-to-all-start.2) | async-done | bytes 110624 | tf_op jit(solution)/shard_map/all_to_all | solution.py:27
  125.5 0.2 reshape.99
  125.7 0.2 copy.113
  125.9 0.2 div.14
  126.1 0.8 copy.116
  (14 shorter events, 0.2 us)
Async XLA Ops:
  0.6 21.4 %copy-start = (bf16[64,32,3,3,3]{0,1,4,3,2:T(8,128)(2,1)S(1)}, bf16[64,32,3,3,3]{0,1,4,3,2:T(8,128)(2,1)}, u32[]{:S(2)}) copy-start(bf16[64,32,3,3,3]{0,1,4,3,2:T(8,128)(2,1)} %param.6) | copy-start | bytes 331780
  1.6 13.6 %collective-permute-start = (bf16[1,32,1,16,128]{4,3,2,1,0:T(8,128)(2,1)S(1)}, bf16[1,32,1,16,128]{4,3,2,1,0:T(8,128)(2,1)S(1)}, u32[]{:S(2)}, u32[]{:S(2)}) collective-permute-start(bf16[1,32,1,16,128]{4,3,2,1,0:T(8,128)(2,1)S(1)} %slice.40), channel_id=1, source_target_pairs={{0,1},{1,2},{2,3},{3,4},{4,5},{5,6},{6,7},{7,8},{8,9},{9,10},{10,1... | collective-permute-start | bytes 393224 | tf_op jit(solution)/shard_map/ppermute | solution.py:10
  21.3 0.8 copy-start.3
  22.1 1.9 %copy-start.1 = (bf16[1,32,3,16,128]{1,0,4,3,2:T(2,128)(2,1)S(1)}, bf16[1,32,3,16,128]{1,0,4,3,2:T(2,128)(2,1)}, u32[]{:S(2)}) copy-start(bf16[1,32,3,16,128]{1,0,4,3,2:T(2,128)(2,1)} %copy.107) | copy-start | bytes 1179652
  30.5 28.5 %copy-start.2 = (pred[8,18]{0,1:T(8,128)(4,1)S(1)}, pred[8,18]{0,1:T(8,128)(4,1)}, u32[]{:S(2)}) copy-start(pred[8,18]{0,1:T(8,128)(4,1)} %constant.57) | copy-start | bytes 436
  31.9 51.7 %all-to-all-start = ((f32[64,1,864]{2,1,0:T(1,128)}), f32[64,1,864]{2,1,0:T(1,128)S(1)}, u32[]{:S(2)}, u32[]{:S(2)}) async-start(f32[64,1,864]{2,1,0:T(1,128)} %copy.110), calls=%async_computation | async-start | bytes 458752 | tf_op jit(solution)/shard_map/all_to_all | solution.py:21
  56.3 34.2 %collective-permute-start.1 = (bf16[1,64,1,8,64]{1,3,4,0,2:T(8,128)(2,1)S(1)}, bf16[1,64,1,8,64]{1,3,4,0,2:T(8,128)(2,1)S(1)}, u32[]{:S(2)}, u32[]{:S(2)}) collective-permute-start(bf16[1,64,1,8,64]{1,3,4,0,2:T(8,128)(2,1)S(1)} %fusion.17), channel_id=1, source_target_pairs={{1,0},{2,1},{3,2},{4,3},{5,4},{6,5},{7,6},{8,7},{9,8},{10,9},{11,1... | collective-permute-start | bytes 196616 | tf_op jit(solution)/shard_map/ppermute | solution.py:10
  84.4 11.0 %all-to-all-start.1 = ((f32[16,1,864]{2,1,0:T(1,128)}), f32[16,1,864]{2,1,0:T(1,128)S(1)}, u32[]{:S(2)}, u32[]{:S(2)}) async-start(f32[16,1,864]{2,1,0:T(1,128)} %broadcast_in_dim.6), calls=%async_computation.1 | async-start | bytes 114688 | tf_op jit(solution)/shard_map/all_to_all | solution.py:27
  98.3 27.2 %all-to-all-start.2 = ((bf16[64,2,432]{2,1,0:T(2,128)(2,1)}), bf16[64,2,432]{2,1,0:T(2,128)(2,1)S(1)}, u32[]{:S(2)}, u32[]{:S(2)}) async-start(bf16[64,2,432]{2,1,0:T(2,128)(2,1)} %reshape.98), calls=%async_computation.2 | async-start | bytes 262144 | tf_op jit(solution)/shard_map/all_to_all | solution.py:27
